TPU v7x, 512 devices: a whole 4x4x16 slice. The times are simulated.
512 devices in a mesh: fsdp: 128 (over z, y, core), seq: 4 (over x).
Axes of the slice: x: 4, y: 4, z: 16, core: 2. Of those that a mesh axis runs over, the one named last changes fastest.
Arguments:
- tokens: bfloat16 [128, 512, 8192], P('fsdp', 'seq'), may hold values from -6 to 6
- queries: bfloat16 [128, 512, 8192], P('fsdp', None, 'seq'), may hold values from -6 to 6
- key_weight: bfloat16 [8192, 1024], P('fsdp', 'seq'), may hold values from -1 to 1
- u_factor: float32 [8192, 64], P('fsdp'), may hold values from -6 to 6
- v_factor: float32 [1024, 64], replicated, may hold values from -6 to 6
Outputs:
- update: float32 [8192, 1024], P('fsdp')
- losses: float32 [2], replicated
All inputs are finite; a program needn't handle non-finite values.
Results may differ from a plain program's by a relative error of at most 0.0003.
Values may be sent and summed in bfloat16 or wider, within the bound.
No kernel may reach another device: no remote copies, remote signals or barrier semaphores. Data moves between devices by JAX's collectives and lax.ppermute only.
A program may use at most 64 MiB of HBM per device.

v0:
```python
import math

import jax
import jax.numpy as jnp
from jax import lax
from jax.sharding import PartitionSpec as P

D = 8192
HQ = 64
HD = 128
R = 64
KD = 1024
GROUP = 8


def highest(left, right):
    return jnp.dot(left, right, precision=lax.Precision.HIGHEST, preferred_element_type=jnp.float32)


def solve_rows(rows, gram):
    lower = jnp.linalg.cholesky(gram)
    return lax.linalg.triangular_solve(lower, rows, left_side=False, lower=True, transpose_a=True)


def local(tokens, queries, key_weight, u_factor, v_factor):
    q_v = v_factor
    for turn in range(2):
        q_v = solve_rows(q_v, highest(q_v.T, q_v))
    u_rows = u_factor
    for turn in range(2):
        whole_u = lax.all_gather(u_rows, "fsdp", axis=0, tiled=True)
        u_rows = solve_rows(u_rows, highest(whole_u.T, whole_u))
    q_low = u_rows.astype(jnp.bfloat16)
    whole_x = lax.all_gather(tokens, "seq", axis=1, tiled=True)[0]
    length = whole_x.shape[0]
    slice_width = key_weight.shape[1]
    weight_piece = lax.all_gather(key_weight, "fsdp", axis=0, tiled=True)
    factor_piece = lax.all_gather(q_low, "fsdp", axis=0, tiled=True)
    base = jnp.dot(whole_x, weight_piece, preferred_element_type=jnp.float32)
    side = jnp.dot(whole_x, factor_piece, preferred_element_type=jnp.float32)
    col_start = lax.axis_index("seq") * slice_width
    v_slice = lax.dynamic_slice_in_dim(q_v, col_start, slice_width, 0)
    offset = 2.0 * highest(side, v_slice.T)
    keys = jnp.stack([base + offset, base - offset]).astype(jnp.bfloat16)
    local_kv = slice_width // HD
    query_rows = queries[0]
    query_heads = query_rows.reshape(length, local_kv, GROUP, HD).transpose(1, 2, 0, 3)
    key_heads = keys.reshape(2, length, local_kv, HD).transpose(2, 0, 1, 3)
    places = jnp.arange(length)
    causal = places[:, None] >= places[None, :]
    factor_scale = 1.0 / math.sqrt(HD)

    def one_query_head(query_one, key_one):
        scores = (
            jnp.einsum("td,npd->ntp", query_one, key_one, preferred_element_type=jnp.float32)
            * factor_scale
        )
        scores = jnp.where(causal[None], scores, -1e30)
        top = jnp.max(scores, axis=-1)
        total = jnp.sum(jnp.where(causal[None], jnp.exp(scores - top[..., None]), 0.0), axis=-1)
        return jnp.sum(top + jnp.log(total), axis=1)

    def one_key_head(pair):
        group_queries, key_one = pair
        return jnp.sum(
            lax.map(lambda query_one: one_query_head(query_one, key_one), group_queries), axis=0
        )

    partial_sums = jnp.sum(lax.map(one_key_head, (query_heads, key_heads)), axis=0)
    sums = lax.psum(partial_sums, ("fsdp", "seq"))
    losses = sums / (lax.axis_size("fsdp") * length * HQ)
    unit = math.sqrt(D * KD / R)
    update = unit * highest(u_rows, q_v.T)
    return (update, losses)


def solution(mesh):
    in_specs = (
        P("fsdp", "seq", None),
        P("fsdp", None, "seq"),
        P("fsdp", "seq"),
        P("fsdp", None),
        P(),
    )
    out_specs = (P("fsdp", None), P())
    return jax.shard_map(local, mesh=mesh, in_specs=in_specs, out_specs=out_specs, check_vma=False)
```

profile of v0, /device:TPU:1, one launch (start us, length us, event | category | flops | bytes accessed | tf_op | source)
XLA Modules:
  0.0 858.6 jit_solution(16340279235827252313)
XLA Ops:
  7.2 0.7 all-gather.6.cloned.1.call-update
  8.0 151.0 %all-gather.6.cloned.1.call-done = f32[8192,64]{1,0:T(8,128)} async-done(((f32[64,64]{1,0:T(8,128)}), f32[8192,64]{1,0:T(8,128)}) %all-gather.6.cloned.1.call-update) | async-done | bytes 2097168 | tf_op jit(solution)/shard_map/all_gather | solution.py:31
  159.0 10.4 %fusion.30 = f32[64,64]{1,0:T(8,128)S(1)} fusion(f32[8192,64]{1,0:T(8,128)} %all-gather.6.cloned.1.call-done), kind=kOutput, calls=%fused_computation.63 | convolution fusion | flops 402653184 | bytes 2113536 | tf_op jit(solution)/shard_map/dot_general | solution.py:17
  169.5 5.8 cholesky.74
  176.1 0.7 fusion.14
  176.7 4.9 custom-call.10
  181.9 0.7 copy.22
  182.8 137.7 %all-gather.8.cloned.1.call-done = f32[8192,64]{1,0:T(8,128)} async-done(((f32[64,64]{1,0:T(8,128)}), f32[8192,64]{1,0:T(8,128)}) %all-gather.8.cloned.1.call-update) | async-done | bytes 2097168 | tf_op jit(solution)/shard_map/all_gather | solution.py:31
  320.6 10.4 %fusion.31 = f32[64,64]{1,0:T(8,128)S(1)} fusion(f32[8192,64]{1,0:T(8,128)} %all-gather.8.cloned.1.call-done), kind=kOutput, calls=%fused_computation.64 | convolution fusion | flops 402653184 | bytes 2113536 | tf_op jit(solution)/shard_map/dot_general | solution.py:17
  331.1 5.8 cholesky.85
  337.6 0.7 fusion.15
  338.3 4.9 custom-call.11
  343.4 0.7 copy.27
  345.8 5.8 cholesky.96
  353.0 4.9 custom-call.12
  358.8 5.9 cholesky.107
  366.0 4.9 custom-call.13
  370.9 2.8 copy.26
  374.1 107.1 %all-gather.14.cloned.1.call-done = bf16[8192,64]{1,0:T(8,128)(2,1)} async-done(((bf16[64,64]{1,0:T(8,128)(2,1)}), bf16[8192,64]{1,0:T(8,128)(2,1)}) %all-gather.14.cloned.1.call-update) | async-done | bytes 1048592 | tf_op jit(solution)/shard_map/all_gather | solution.py:38
  481.1 88.4 %all-gather.10.cloned.1.call-done = bf16[1,512,8192]{2,1,0:T(8,128)(2,1)} async-done(((bf16[1,128,8192]{2,1,0:T(8,128)(2,1)}), bf16[1,512,8192]{2,1,0:T(8,128)(2,1)}) %all-gather.10.cloned.1.call-update) | async-done | bytes 8388624 | tf_op jit(solution)/shard_map/all_gather | solution.py:34
  569.6 6.7 fusion.9
  576.9 139.4 %all-gather.12.cloned.1.call-done = bf16[8192,256]{1,0:T(8,128)(2,1)} async-done(((bf16[64,256]{1,0:T(8,128)(2,1)}), bf16[8192,256]{1,0:T(8,128)(2,1)}) %all-gather.12.cloned.1.call-update) | async-done | bytes 4194320 | tf_op jit(solution)/shard_map/all_gather | solution.py:37
  716.3 6.9 add_convert_fusion
  723.7 25.3 %while.26 = (s32[]{:T(128)}, f32[2,2]{1,0:T(2,128)S(1)}, bf16[2,8,512,128]{2,3,1,0:T(8,128)(2,1)}, bf16[2,2,512,128]{3,2,1,0:T(8,128)(2,1)S(1)}, s32[]{:T(128)},...) while((s32[]{:T(128)}, f32[2,2]{1,0:T(2,128)S(1)}, ...), condition=%wide.region_9.13_spmd.clone.clone, body=%wide.region_2.12_spmd.clone.clone.sunk | while | flops 138674192 | bytes 10113394 | solution.py:69
  723.7 1.3 constant_dynamic-slice_fusion.2
  725.0 0.7 copy.33
  725.8 10.4 %while.27 = (s32[]{:T(128)}, f32[8,2]{1,0:T(8,128)S(1)}, pred[512,512]{0,1:T(8,128)(4,1)S(1)}, bf16[8,512,128]{2,1,0:T(8,128)(2,1)S(1)}, bf16[2,512,128]{2,1,0:T(8,128)(2,1)S(1)}, /*index=5*/s32[]{:T(128)}, s32[]{:T(128)}) while((s32[]{:T(128)}, f32[8,2]{1,0:T(8,128)S(1)}, pred[512,512]{0,1:T(8,128)(4,1)S(1)}, ...), condition=%wide.region_7.10_spmd.clone, body=%wide.region_3.9_spmd.clone.sunk | while | flops 138412032 | bytes 5132397 | solution.py:66
  736.3 1.3 constant_dynamic-slice_fusion.2
  737.7 0.7 copy.33
  738.5 10.4 %while.27 = (s32[]{:T(128)}, f32[8,2]{1,0:T(8,128)S(1)}, pred[512,512]{0,1:T(8,128)(4,1)S(1)}, bf16[8,512,128]{2,1,0:T(8,128)(2,1)S(1)}, bf16[2,512,128]{2,1,0:T(8,128)(2,1)S(1)}, /*index=5*/s32[]{:T(128)}, s32[]{:T(128)}) while((s32[]{:T(128)}, f32[8,2]{1,0:T(8,128)S(1)}, pred[512,512]{0,1:T(8,128)(4,1)S(1)}, ...), condition=%wide.region_7.10_spmd.clone, body=%wide.region_3.9_spmd.clone.sunk | while | flops 138412032 | bytes 5132397 | solution.py:66
  749.0 1.1 convolution_multiply_fusion.1
  750.1 101.5 %psum.7 = f32[2]{0:T(128)S(1)} all-reduce(f32[2]{0:T(128)S(1)} %reduce_sum.36), channel_id=1, replica_groups=mesh['fsdp'=128,'seq'=4] {'fsdp','seq'}, use_global_device_ids=true, to_apply=%region_11.15 | all-reduce | flops 2 | bytes 16 | tf_op jit(solution)/shard_map/psum | solution.py:70
  (120 shorter events, 30.4 us)
Async XLA Ops:
  7.2 338.2 %copy-start = (f32[1024,64]{0,1:T(8,128)S(1)}, f32[1024,64]{0,1:T(8,128)}, u32[]{:S(2)}) copy-start(f32[1024,64]{0,1:T(8,128)} %param.18) | copy-start | bytes 786436
  7.2 151.8 %all-gather.6.cloned.1.call-start = ((), (), s32[]{:S(2)}) async-start(), calls=%async_computation | async-start | bytes 4227072 | tf_op jit(solution)/shard_map/all_gather | solution.py:31
  7.9 173.7 %copy-start.2 = (f32[64,64]{1,0:T(8,128)S(1)}, f32[64,64]{1,0:T(8,128)}, u32[]{:S(2)}) copy-start(f32[64,64]{1,0:T(8,128)} %param.17) | copy-start | bytes 49156
  7.9 312.6 %all-gather.8.cloned.1.call-start = ((), (), s32[]{:S(2)}) async-start(), calls=%async_computation.1 | async-start | bytes 4227072 | tf_op jit(solution)/shard_map/all_gather | solution.py:31
  182.6 298.5 %all-gather.14.cloned.1.call-start = ((), (), s32[]{:S(2)}) async-start(), calls=%async_computation.4 | async-start | bytes 2113536 | tf_op jit(solution)/shard_map/all_gather | solution.py:38
  344.2 26.7 %copy-start.1 = (bf16[1,512,2048]{2,1,0:T(8,128)(2,1)S(1)}, bf16[1,512,2048]{2,1,0:T(8,128)(2,1)}, u32[]{:S(2)}) copy-start(bf16[1,512,2048]{2,1,0:T(8,128)(2,1)} %param.15) | copy-start | bytes 6291460
  344.2 225.4 %all-gather.10.cloned.1.call-start = ((), (), s32[]{:S(2)}) async-start(), calls=%async_computation.2 | async-start | bytes 10485760 | tf_op jit(solution)/shard_map/all_gather | solution.py:34
  344.7 371.6 %all-gather.12.cloned.1.call-start = ((), (), s32[]{:S(2)}) async-start(), calls=%async_computation.3 | async-start | bytes 4227072 | tf_op jit(solution)/shard_map/all_gather | solution.py:37
Sparse Core Ops, SparseCore 0:
  11.1 147.8 all-gather.5
  182.7 137.7 all-gather.7
  344.3 136.8 all-gather.13
  483.1 86.4 all-gather.9
  572.5 143.6 all-gather.11
where the time goes:
time: 859 us
  waiting for transfers between devices  625 us (73%)
  blocking collectives  101 us (12%)
  other arithmetic  60.3 us (7%)
  matrix products  47.2 us (5%)
  between operations  14 us (2%)
  local copies, waits for them, and re-layouts  9.49 us (1%)
    all_gather x2, waiting for transfers between devices, local(): whole_u = lax.all_gather(u_rows, 'fsdp', axis=0, tiled=True)  289 us
    all_gather x1, waiting for transfers between devices, local(): weight_piece = lax.all_gather(key_weight, 'fsdp', axis=0, tiled=True)  139 us
    all_gather x1, waiting for transfers between devices, local(): factor_piece = lax.all_gather(q_low, 'fsdp', axis=0, tiled=True)  107 us
    psum x1, blocking collectives, local(): sums = lax.psum(partial_sums, ('fsdp', 'seq'))  101 us
    all_gather x1, waiting for transfers between devices, local(): whole_x = lax.all_gather(tokens, 'seq', axis=1, tiled=True)[0]  88.4 us
    another operation x12, other arithmetic, solve_rows(): lower = jnp.linalg.cholesky(gram)  26.1 us
    dot_general x6, matrix products, highest(): jnp.dot(left, right, precision=lax.Precision.HIGHEST, preferred_element_t...  23.4 us
    another operation x8, other arithmetic, solve_rows(): lax.linalg.triangular_solve(lower, rows, left_side=False, lower=True, tra...  22.2 us
  transfers between devices with their start and end apart: 5, of which 5 were waited for; matrix products, arithmetic and copies ran while one was open for 4% of the time, Pallas kernels for 0%

commit v1 on v0

--- a/solution.py
+++ b/solution.py
@@ -22,32 +22,68 @@
     return lax.linalg.triangular_solve(lower, rows, left_side=False, lower=True, transpose_a=True)
 
 
+def orthonormal(factor):
+    for turn in range(2):
+        factor = solve_rows(factor, highest(factor.T, factor))
+    return factor
+
+
+def split3(values):
+    hi = lax.reduce_precision(values, exponent_bits=8, mantissa_bits=7)
+    rest = values - hi
+    mid = lax.reduce_precision(rest, exponent_bits=8, mantissa_bits=7)
+    lo = rest - mid
+    return [piece.astype(jnp.bfloat16) for piece in (hi, mid, lo)]
+
+
 def local(tokens, queries, key_weight, u_factor, v_factor):
-    q_v = v_factor
-    for turn in range(2):
-        q_v = solve_rows(q_v, highest(q_v.T, q_v))
-    u_rows = u_factor
-    for turn in range(2):
-        whole_u = lax.all_gather(u_rows, "fsdp", axis=0, tiled=True)
-        u_rows = solve_rows(u_rows, highest(whole_u.T, whole_u))
-    q_low = u_rows.astype(jnp.bfloat16)
-    whole_x = lax.all_gather(tokens, "seq", axis=1, tiled=True)[0]
-    length = whole_x.shape[0]
+    n_seq = lax.axis_size("seq")
+    me_seq = lax.axis_index("seq")
+    me_fsdp = lax.axis_index("fsdp")
     slice_width = key_weight.shape[1]
-    weight_piece = lax.all_gather(key_weight, "fsdp", axis=0, tiled=True)
-    factor_piece = lax.all_gather(q_low, "fsdp", axis=0, tiled=True)
-    base = jnp.dot(whole_x, weight_piece, preferred_element_type=jnp.float32)
-    side = jnp.dot(whole_x, factor_piece, preferred_element_type=jnp.float32)
-    col_start = lax.axis_index("seq") * slice_width
+    rows = u_factor.shape[0]
+
+    packed = jnp.concatenate([key_weight] + split3(u_factor), axis=1)
+    whole = lax.all_gather(packed, "fsdp", axis=0, tiled=True)
+
+    x_local = tokens[0]
+    chunk = x_local.shape[0]
+    chunks = [x_local]
+    for shift in range(1, n_seq):
+        chunks.append(lax.ppermute(x_local, "seq", [(i, (i + shift) % n_seq) for i in range(n_seq)]))
+
+    q_v = orthonormal(v_factor)
+    weight_piece = whole[:, :slice_width]
+    r = u_factor.shape[1]
+    u_whole = (
+        whole[:, slice_width : slice_width + r].astype(jnp.float32)
+        + whole[:, slice_width + r : slice_width + 2 * r].astype(jnp.float32)
+    ) + whole[:, slice_width + 2 * r :].astype(jnp.float32)
+    q_u = orthonormal(u_whole)
+    q_low = q_u.astype(jnp.bfloat16)
+    both = jnp.concatenate([weight_piece, q_low], axis=1)
+
+    col_start = me_seq * slice_width
     v_slice = lax.dynamic_slice_in_dim(q_v, col_start, slice_width, 0)
-    offset = 2.0 * highest(side, v_slice.T)
-    keys = jnp.stack([base + offset, base - offset]).astype(jnp.bfloat16)
+    key_parts = []
+    for part in chunks:
+        prod = jnp.dot(part, both, preferred_element_type=jnp.float32)
+        base = prod[:, :slice_width]
+        side = prod[:, slice_width:]
+        offset = 2.0 * highest(side, v_slice.T)
+        key_parts.append(jnp.stack([base + offset, base - offset]).astype(jnp.bfloat16))
+    keys = jnp.concatenate(key_parts, axis=1)
+    length = keys.shape[1]
+
+    block = (me_seq - jnp.arange(n_seq)) % n_seq
+    key_pos = (block[:, None] * chunk + jnp.arange(chunk)[None, :]).reshape(length)
+
     local_kv = slice_width // HD
     query_rows = queries[0]
     query_heads = query_rows.reshape(length, local_kv, GROUP, HD).transpose(1, 2, 0, 3)
     key_heads = keys.reshape(2, length, local_kv, HD).transpose(2, 0, 1, 3)
     places = jnp.arange(length)
-    causal = places[:, None] >= places[None, :]
+    causal = places[:, None] >= key_pos[None, :]
     factor_scale = 1.0 / math.sqrt(HD)
 
     def one_query_head(query_one, key_one):
@@ -70,6 +106,7 @@
     sums = lax.psum(partial_sums, ("fsdp", "seq"))
     losses = sums / (lax.axis_size("fsdp") * length * HQ)
     unit = math.sqrt(D * KD / R)
+    u_rows = lax.dynamic_slice_in_dim(q_u, me_fsdp * rows, rows, 0)
     update = unit * highest(u_rows, q_v.T)
     return (update, losses)
 

time: 859 us -> 375 us (0.44)
  waiting for transfers between devices: 625 us -> 114 us
  starting transfers between devices: 0.38 us -> 12 us
  matrix products: 47.2 us -> 56.9 us
    all_gather x5 -> x1, waiting for transfers between devices: 624 us -> 114 us  [local(): whole = lax.all_gather(packed, 'fsdp', axis=0, tiled=True)]
    ppermute x0 -> x3, starting transfers between devices: none -> 12 us  [local(): lax.ppermute(x_local, 'seq', [(i, (i + shift) % n_seq) for i in range(n_s...]
    another operation x4, matrix products: 1.32 us -> 12.6 us  [solve_rows(): lax.linalg.triangular_solve(lower, rows, left_side=False, lower=True, tra...]
    dot_general x6 -> x9, matrix products: 23.4 us -> 19.6 us  [highest(): jnp.dot(left, right, precision=lax.Precision.HIGHEST, preferred_element_t...]
  transfers between devices with their start and end apart: 5 -> 4, of which waited for: 5 -> 1; matrix products, arithmetic and copies ran while one was open for 4% -> 26% of each run, Pallas kernels for 0% -> 0%
where the time goes in v1:
time: 375 us
  waiting for transfers between devices  114 us (30%)
  blocking collectives  100 us (27%)
  other arithmetic  63 us (17%)
  matrix products  56.9 us (15%)
  between operations  14.4 us (4%)
  local copies, waits for them, and re-layouts  13.9 us (4%)
  starting transfers between devices  12 us (3%)
    all_gather x1, waiting for transfers between devices, local(): whole = lax.all_gather(packed, 'fsdp', axis=0, tiled=True)  114 us
    psum x1, blocking collectives, local(): sums = lax.psum(partial_sums, ('fsdp', 'seq'))  100 us
    another operation x12, other arithmetic, solve_rows(): lower = jnp.linalg.cholesky(gram)  26.1 us
    another operation x8, other arithmetic, solve_rows(): lax.linalg.triangular_solve(lower, rows, left_side=False, lower=True, tra...  22.2 us
    dot_general x9, matrix products, highest(): jnp.dot(left, right, precision=lax.Precision.HIGHEST, preferred_element_t...  19.6 us
    dot_general x4, matrix products, local(): prod = jnp.dot(part, both, preferred_element_type=jnp.float32)  15.9 us
    another operation x4, matrix products, solve_rows(): lax.linalg.triangular_solve(lower, rows, left_side=False, lower=True, tra...  12.6 us
    ppermute x3, starting transfers between devices, local(): lax.ppermute(x_local, 'seq', [(i, (i + shift) % n_seq) for i in range(n_s...  12 us
  transfers between devices with their start and end apart: 4, of which 1 were waited for; matrix products, arithmetic and copies ran while one was open for 26% of the time, Pallas kernels for 0%

profile of v1, /device:TPU:1, one launch (start us, length us, event | category | flops | bytes accessed | tf_op | source)
XLA Modules:
  0.0 374.8 jit_solution(791632605691923865)
XLA Ops:
  8.2 1.5 pad_maximum_fusion.1
  9.7 5.5 %collective-permute-start.1 = (bf16[128,8192]{1,0:T(8,128)(2,1)}, bf16[128,8192]{1,0:T(8,128)(2,1)}, u32[]{:S(2)}, u32[]{:S(2)}) collective-permute-start(bf16[128,8192]{1,0:T(8,128)(2,1)} %bitcast.134), channel_id=1, source_target_pairs={{0,2},{1,3},{2,0},{3,1},{4,6},{5,7},{6,4},{7,5},{8,10},{9,11},{10,... | collective-permute-start | bytes 6291464 | tf_op jit(solution)/shard_map/ppermute | solution.py:53
  15.1 2.2 collective-permute-start
  17.4 4.3 %collective-permute-start.2 = (bf16[128,8192]{1,0:T(8,128)(2,1)}, bf16[128,8192]{1,0:T(8,128)(2,1)}, u32[]{:S(2)}, u32[]{:S(2)}) collective-permute-start(bf16[128,8192]{1,0:T(8,128)(2,1)} %bitcast.136), channel_id=1, source_target_pairs={{0,3},{1,0},{2,1},{3,2},{4,7},{5,4},{6,5},{7,6},{8,11},{9,8},{10,9... | collective-permute-start | bytes 6291464 | tf_op jit(solution)/shard_map/ppermute | solution.py:53
  22.1 5.8 %cholesky.96 = f32[64,64]{1,0:T(8,128)S(1)} custom-call(f32[64,64]{1,0:T(8,128)S(1)} %fusion.32), custom_call_target="Cholesky" | custom-call | tf_op jit(solution)/shard_map/jit(cholesky)/cholesky | solution.py:21
  29.3 4.9 %custom-call.12 = f32[1,64,64]{1,2,0:T(8,128)S(1)} custom-call(f32[1,64,64]{2,1,0:T(8,128)S(1)} %fusion.22), custom_call_target="InvertDiagBlocksLowerTriangular" | custom-call | tf_op jit(solution)/shard_map/triangular_solve/custom-call.2 | solution.py:22
  35.1 5.9 %cholesky.107 = f32[64,64]{1,0:T(8,128)S(1)} custom-call(f32[64,64]{1,0:T(8,128)S(1)} %fusion.30), custom_call_target="Cholesky" | custom-call | tf_op jit(solution)/shard_map/jit(cholesky)/cholesky | solution.py:21
  42.3 4.9 %custom-call.13 = f32[1,64,64]{1,2,0:T(8,128)S(1)} custom-call(f32[1,64,64]{2,1,0:T(8,128)S(1)} %fusion.23), custom_call_target="InvertDiagBlocksLowerTriangular" | custom-call | tf_op jit(solution)/shard_map/triangular_solve/custom-call.2 | solution.py:22
  47.2 2.7 copy.28
  50.0 1.1 convolution_bitcast_fusion.2
  51.1 113.6 %all-gather.2.cloned.1.call-done = bf16[8192,448]{1,0:T(8,128)(2,1)} async-done(((bf16[64,448]{1,0:T(8,128)(2,1)}), bf16[8192,448]{1,0:T(8,128)(2,1)}) %all-gather.2.cloned.1.call-update) | async-done | bytes 7340048 | tf_op jit(solution)/shard_map/all_gather | solution.py:47
  164.8 13.3 %fusion.9 = f32[64,64]{1,0:T(8,128)S(1)} fusion(bf16[8192,448]{1,0:T(8,128)(2,1)} %all-gather.2.cloned.1.call-done), kind=kOutput, calls=%fused_computation.19 | convolution fusion | flops 405274624 | bytes 6307840 | tf_op jit(solution)/shard_map/dot_general | solution.py:17
  178.2 5.8 %cholesky.74 = f32[64,64]{1,0:T(8,128)S(1)} custom-call(f32[64,64]{1,0:T(8,128)S(1)} %fusion.36), custom_call_target="Cholesky" | custom-call | tf_op jit(solution)/shard_map/jit(cholesky)/cholesky | solution.py:21
  185.4 4.9 %custom-call.10 = f32[1,64,64]{1,2,0:T(8,128)S(1)} custom-call(f32[1,64,64]{2,1,0:T(8,128)S(1)} %fusion.20), custom_call_target="InvertDiagBlocksLowerTriangular" | custom-call | tf_op jit(solution)/shard_map/triangular_solve/custom-call.0 | solution.py:22
  190.3 7.8 %convolution_bitcast_fusion.1 = f32[8192,64]{0,1:T(8,128)S(1)} fusion(bf16[8192,448]{1,0:T(8,128)(2,1)} %all-gather.2.cloned.1.call-done, f32[1,64,64]{1,2,0:T(8,128)S(1)} %custom-call.10), kind=kOutput, calls=%fused_computation.16 | convolution fusion | flops 405274624 | bytes 8404992 | tf_op jit(solution)/shard_map/triangular_solve/dot.16 | solution.py:22
  198.0 1.8 fusion.49
  199.9 5.8 %cholesky.85 = f32[64,64]{1,0:T(8,128)S(1)} custom-call(f32[64,64]{1,0:T(8,128)S(1)} %fusion.34), custom_call_target="Cholesky" | custom-call | tf_op jit(solution)/shard_map/jit(cholesky)/cholesky | solution.py:21
  207.1 4.9 %custom-call.11 = f32[1,64,64]{1,2,0:T(8,128)S(1)} custom-call(f32[1,64,64]{2,1,0:T(8,128)S(1)} %fusion.21), custom_call_target="InvertDiagBlocksLowerTriangular" | custom-call | tf_op jit(solution)/shard_map/triangular_solve/custom-call.0 | solution.py:22
  212.0 3.3 fusion.48
  215.3 1.8 copy.29
  217.1 2.6 slice.59
  220.6 1.9 convolution_bitcast_fusion.7
  223.2 4.7 %convolution_bitcast_fusion.5 = f32[128,320]{0,1:T(8,128)S(1)} fusion(bf16[128,8192]{1,0:T(8,128)(2,1)} %collective-permute-done.1, bf16[8192,64]{1,0:T(8,128)(2,1)S(1)} %copy-done.3, bf16[8192,256]{1,0:T(8,128)(2,1)} %copy-done.1), kind=kOutput, calls=%fused_computation.30 | convolution fusion | flops 681574400 | bytes 7503872 | tf_op jit(solution)/shard_map/dot_general | solution.py:70
  228.6 4.7 %convolution_bitcast_fusion.6 = f32[128,320]{0,1:T(8,128)S(1)} fusion(bf16[128,8192]{1,0:T(8,128)(2,1)} %collective-permute-done, bf16[8192,64]{1,0:T(8,128)(2,1)S(1)} %copy-done.3, bf16[8192,256]{1,0:T(8,128)(2,1)} %copy-done.1), kind=kOutput, calls=%fused_computation.31 | convolution fusion | flops 681574400 | bytes 7503872 | tf_op jit(solution)/shard_map/dot_general | solution.py:70
  233.9 4.7 %convolution_bitcast_fusion.4 = f32[128,320]{0,1:T(8,128)S(1)} fusion(bf16[128,8192]{1,0:T(8,128)(2,1)} %collective-permute-done.2, bf16[8192,64]{1,0:T(8,128)(2,1)S(1)} %copy-done.3, bf16[8192,256]{1,0:T(8,128)(2,1)} %copy-done.1), kind=kOutput, calls=%fused_computation.29 | convolution fusion | flops 681574400 | bytes 7503872 | tf_op jit(solution)/shard_map/dot_general | solution.py:70
  239.3 25.5 %while.23 = (s32[]{:T(128)}, f32[2,2]{1,0:T(2,128)S(1)}, bf16[2,8,512,128]{2,3,1,0:T(8,128)(2,1)}, bf16[2,2,512,128]{3,2,1,0:T(8,128)(2,1)S(1)}, s32[512]{0:T(51...) while((s32[]{:T(128)}, f32[2,2]{1,0:T(2,128)S(1)}, ...), condition=%wide.region_9.13_spmd.clone, body=%wide.region_2.12_spmd.clone.sunk | while | flops 138674192 | bytes 10115466 | solution.py:105
  239.6 1.3 constant_dynamic-slice_fusion.2
  241.6 10.4 %while.24 = (s32[]{:T(128)}, f32[8,2]{1,0:T(8,128)S(1)}, pred[512,512]{0,1:T(8,128)(4,1)S(1)}, bf16[8,512,128]{2,1,0:T(8,128)(2,1)S(1)}, bf16[2,512,128]{2,1,0:T(8,128)(2,1)S(1)}, /*index=5*/s32[]{:T(128)}, s32[]{:T(128)}) while((s32[]{:T(128)}, f32[8,2]{1,0:T(8,128)S(1)}, pred[512,512]{0,1:T(8,128)(4,1)S(1)}, ...), condition=%wide.region_7.10_spmd, body=%wide.region_3.0_spmd.sunk | while | flops 138412032 | bytes 5132405 | solution.py:102
  252.3 1.3 constant_dynamic-slice_fusion.2
  254.4 10.4 %while.24 = (s32[]{:T(128)}, f32[8,2]{1,0:T(8,128)S(1)}, pred[512,512]{0,1:T(8,128)(4,1)S(1)}, bf16[8,512,128]{2,1,0:T(8,128)(2,1)S(1)}, bf16[2,512,128]{2,1,0:T(8,128)(2,1)S(1)}, /*index=5*/s32[]{:T(128)}, s32[]{:T(128)}) while((s32[]{:T(128)}, f32[8,2]{1,0:T(8,128)S(1)}, pred[512,512]{0,1:T(8,128)(4,1)S(1)}, ...), condition=%wide.region_7.10_spmd, body=%wide.region_3.0_spmd.sunk | while | flops 138412032 | bytes 5132405 | solution.py:102
  264.8 100.5 %psum.7 = f32[2]{0:T(128)S(1)} all-reduce(f32[2]{0:T(128)S(1)} %reduce_sum.36), channel_id=1, replica_groups=mesh['fsdp'=128,'seq'=4] {'fsdp','seq'}, use_global_device_ids=true, to_apply=%region_11.15 | all-reduce | flops 2 | bytes 16 | tf_op jit(solution)/shard_map/psum | solution.py:106
  365.8 2.2 convolution_multiply_fusion
  (135 shorter events, 34.3 us)
Async XLA Ops:
  7.2 14.5 %copy-start = (f32[1024,64]{0,1:T(8,128)S(1)}, f32[1024,64]{0,1:T(8,128)}, u32[]{:S(2)}) copy-start(f32[1024,64]{0,1:T(8,128)} %param.18) | copy-start | bytes 786436
  7.2 40.0 %copy-start.4 = (bf16[1,512,2048]{2,1,0:T(8,128)(2,1)S(1)}, bf16[1,512,2048]{2,1,0:T(8,128)(2,1)}, u32[]{:S(2)}) copy-start(bf16[1,512,2048]{2,1,0:T(8,128)(2,1)} %param.15) | copy-start | bytes 6291460
  7.2 157.6 %all-gather.2.cloned.1.call-start = ((), (), s32[]{:S(2)}) async-start(), calls=%async_computation | async-start | bytes 8454144 | tf_op jit(solution)/shard_map/all_gather | solution.py:47
  9.7 213.5 %collective-permute-start.1 = (bf16[128,8192]{1,0:T(8,128)(2,1)}, bf16[128,8192]{1,0:T(8,128)(2,1)}, u32[]{:S(2)}, u32[]{:S(2)}) collective-permute-start(bf16[128,8192]{1,0:T(8,128)(2,1)} %bitcast.134), channel_id=1, source_target_pairs={{0,2},{1,3},{2,0},{3,1},{4,6},{5,7},{6,4},{7,5},{8,10},{9,11},{10,... | collective-permute-start | bytes 6291464 | tf_op jit(solution)/shard_map/ppermute | solution.py:53
  15.1 213.4 %collective-permute-start = (bf16[128,8192]{1,0:T(8,128)(2,1)}, bf16[128,8192]{1,0:T(8,128)(2,1)}, u32[]{:S(2)}, u32[]{:S(2)}) collective-permute-start(bf16[128,8192]{1,0:T(8,128)(2,1)} %bitcast.135), channel_id=1, source_target_pairs={{0,1},{1,2},{2,3},{3,0},{4,5},{5,6},{6,7},{7,4},{8,9},{9,10},{10,1... | collective-permute-start | bytes 6291464 | tf_op jit(solution)/shard_map/ppermute | solution.py:53
  17.4 216.6 %collective-permute-start.2 = (bf16[128,8192]{1,0:T(8,128)(2,1)}, bf16[128,8192]{1,0:T(8,128)(2,1)}, u32[]{:S(2)}, u32[]{:S(2)}) collective-permute-start(bf16[128,8192]{1,0:T(8,128)(2,1)} %bitcast.136), channel_id=1, source_target_pairs={{0,3},{1,0},{2,1},{3,2},{4,7},{5,4},{6,5},{7,6},{8,11},{9,8},{10,9... | collective-permute-start | bytes 6291464 | tf_op jit(solution)/shard_map/ppermute | solution.py:53
  217.1 2.9 copy-start.3
  217.1 3.5 copy-start.5
  220.6 1.9 copy-start.1
  220.6 1.9 copy-start.2
Sparse Core Ops, SparseCore 0:
  11.7 152.9 all-gather.1

commit v2 on v1

--- a/solution.py
+++ b/solution.py
@@ -36,6 +36,12 @@
     return [piece.astype(jnp.bfloat16) for piece in (hi, mid, lo)]
 
 
+def total_over(values, axis):
+    n = lax.axis_size(axis)
+    spread = jnp.broadcast_to(values[None], (n,) + values.shape)
+    return jnp.sum(lax.all_to_all(spread, axis, 0, 0, tiled=True), axis=0)
+
+
 def local(tokens, queries, key_weight, u_factor, v_factor):
     n_seq = lax.axis_size("seq")
     me_seq = lax.axis_index("seq")
@@ -59,7 +65,7 @@
         whole[:, slice_width : slice_width + r].astype(jnp.float32)
         + whole[:, slice_width + r : slice_width + 2 * r].astype(jnp.float32)
     ) + whole[:, slice_width + 2 * r :].astype(jnp.float32)
-    q_u = orthonormal(u_whole)
+    q_u = orthonormal(lax.optimization_barrier(u_whole))
     q_low = q_u.astype(jnp.bfloat16)
     both = jnp.concatenate([weight_piece, q_low], axis=1)
 
@@ -103,7 +109,7 @@
         )
 
     partial_sums = jnp.sum(lax.map(one_key_head, (query_heads, key_heads)), axis=0)
-    sums = lax.psum(partial_sums, ("fsdp", "seq"))
+    sums = total_over(total_over(partial_sums, "fsdp"), "seq")
     losses = sums / (lax.axis_size("fsdp") * length * HQ)
     unit = math.sqrt(D * KD / R)
     u_rows = lax.dynamic_slice_in_dim(q_u, me_fsdp * rows, rows, 0)

time: 375 us -> 309 us (0.82); the launches traced: 375 us -> 304 us
  blocking collectives: 100 us -> 7.89 us
  waiting for transfers between devices: 114 us -> 127 us
  starting transfers between devices: 12 us -> 21 us
  matrix products: 56.9 us -> 51.2 us
  other arithmetic: 63 us -> 66.9 us
    psum x1 -> x0, blocking collectives: 100 us -> none  [local(): sums = lax.psum(partial_sums, ('fsdp', 'seq'))]
    all_to_all x0 -> x1, waiting for transfers between devices: none -> 12.9 us  [total_over(): return jnp.sum(lax.all_to_all(spread, axis, 0, 0, tiled=True), axis=0)]
    all_to_all x0 -> x1, starting transfers between devices: none -> 9.62 us  [total_over(): return jnp.sum(lax.all_to_all(spread, axis, 0, 0, tiled=True), axis=0)]
    all_to_all x0 -> x1, blocking collectives: none -> 7.89 us  [total_over(): return jnp.sum(lax.all_to_all(spread, axis, 0, 0, tiled=True), axis=0)]
    dot_general x9, matrix products: 19.6 us -> 13.2 us  [highest(): jnp.dot(left, right, precision=lax.Precision.HIGHEST, preferred_element_t...]
    add x0 -> x1, other arithmetic: none -> 3.79 us  [local(): whole[:, slice_width:slice_width + r].astype(jnp.float32) + whole[:, slic...]
  transfers between devices with their start and end apart: 4 -> 5, of which waited for: 1 -> 2; matrix products, arithmetic and copies ran while one was open for 26% -> 32% of each run, Pallas kernels for 0% -> 0%
where the time goes in v2:
time: 309 us; the launch traced here: 304 us
  waiting for transfers between devices  127 us (41%)
  other arithmetic  66.9 us (22%)
  matrix products  51.2 us (17%)
  starting transfers between devices  21 us (7%)
  local copies, waits for them, and re-layouts  14.8 us (5%)
  between operations  14.8 us (5%)
  blocking collectives  7.89 us (3%)
    all_gather x1, waiting for transfers between devices, local(): whole = lax.all_gather(packed, 'fsdp', axis=0, tiled=True)  114 us
    another operation x12, other arithmetic, solve_rows(): lower = jnp.linalg.cholesky(gram)  26.1 us
    another operation x8, other arithmetic, solve_rows(): lax.linalg.triangular_solve(lower, rows, left_side=False, lower=True, tra...  22.2 us
    dot_general x4, matrix products, local(): prod = jnp.dot(part, both, preferred_element_type=jnp.float32)  18 us
    dot_general x9, matrix products, highest(): jnp.dot(left, right, precision=lax.Precision.HIGHEST, preferred_element_t...  13.2 us
    all_to_all x1, waiting for transfers between devices, total_over(): return jnp.sum(lax.all_to_all(spread, axis, 0, 0, tiled=True), axis=0)  12.9 us
    ppermute x3, starting transfers between devices, local(): lax.ppermute(x_local, 'seq', [(i, (i + shift) % n_seq) for i in range(n_s...  11.4 us
    another operation x4, matrix products, solve_rows(): lax.linalg.triangular_solve(lower, rows, left_side=False, lower=True, tra...  11.3 us
  transfers between devices with their start and end apart: 5, of which 2 were waited for; matrix products, arithmetic and copies ran while one was open for 32% of the time, Pallas kernels for 0%

profile of v2, /device:TPU:1, one launch (start us, length us, event | category | flops | bytes accessed | tf_op | source)
XLA Modules:
  0.0 304.0 jit_solution(17268457552491237338)
XLA Ops:
  8.2 1.5 pad_maximum_fusion.1
  9.7 3.9 %collective-permute-start = (bf16[128,8192]{1,0:T(8,128)(2,1)}, bf16[128,8192]{1,0:T(8,128)(2,1)}, u32[]{:S(2)}, u32[]{:S(2)}) collective-permute-start(bf16[128,8192]{1,0:T(8,128)(2,1)} %bitcast.137), channel_id=1, source_target_pairs={{0,1},{1,2},{2,3},{3,0},{4,5},{5,6},{6,7},{7,4},{8,9},{9,10},{10,1... | collective-permute-start | bytes 6291464 | tf_op jit(solution)/shard_map/ppermute | solution.py:59
  13.6 4.4 %collective-permute-start.1 = (bf16[128,8192]{1,0:T(8,128)(2,1)}, bf16[128,8192]{1,0:T(8,128)(2,1)}, u32[]{:S(2)}, u32[]{:S(2)}) collective-permute-start(bf16[128,8192]{1,0:T(8,128)(2,1)} %bitcast.138), channel_id=1, source_target_pairs={{0,2},{1,3},{2,0},{3,1},{4,6},{5,7},{6,4},{7,5},{8,10},{9,11},{10,... | collective-permute-start | bytes 6291464 | tf_op jit(solution)/shard_map/ppermute | solution.py:59
  18.0 3.1 %collective-permute-start.2 = (bf16[128,8192]{1,0:T(8,128)(2,1)}, bf16[128,8192]{1,0:T(8,128)(2,1)}, u32[]{:S(2)}, u32[]{:S(2)}) collective-permute-start(bf16[128,8192]{1,0:T(8,128)(2,1)} %bitcast.139), channel_id=1, source_target_pairs={{0,3},{1,0},{2,1},{3,2},{4,7},{5,4},{6,5},{7,6},{8,11},{9,8},{10,9... | collective-permute-start | bytes 6291464 | tf_op jit(solution)/shard_map/ppermute | solution.py:59
  21.5 5.8 %cholesky.96 = f32[64,64]{1,0:T(8,128)S(1)} custom-call(f32[64,64]{1,0:T(8,128)S(1)} %fusion.25), custom_call_target="Cholesky" | custom-call | tf_op jit(solution)/shard_map/jit(cholesky)/cholesky | solution.py:21
  28.7 4.9 %custom-call.12 = f32[1,64,64]{1,2,0:T(8,128)S(1)} custom-call(f32[1,64,64]{2,1,0:T(8,128)S(1)} %fusion.15), custom_call_target="InvertDiagBlocksLowerTriangular" | custom-call | tf_op jit(solution)/shard_map/triangular_solve/custom-call.2 | solution.py:22
  34.5 5.9 %cholesky.107 = f32[64,64]{1,0:T(8,128)S(1)} custom-call(f32[64,64]{1,0:T(8,128)S(1)} %fusion.23), custom_call_target="Cholesky" | custom-call | tf_op jit(solution)/shard_map/jit(cholesky)/cholesky | solution.py:21
  41.7 4.9 %custom-call.13 = f32[1,64,64]{1,2,0:T(8,128)S(1)} custom-call(f32[1,64,64]{2,1,0:T(8,128)S(1)} %fusion.16), custom_call_target="InvertDiagBlocksLowerTriangular" | custom-call | tf_op jit(solution)/shard_map/triangular_solve/custom-call.2 | solution.py:22
  46.6 2.7 copy.66
  50.5 113.9 %all-gather.2.cloned.1.call-done = bf16[8192,448]{1,0:T(8,128)(2,1)} async-done(((bf16[64,448]{1,0:T(8,128)(2,1)}), bf16[8192,448]{1,0:T(8,128)(2,1)}) %all-gather.2.cloned.1.call-update) | async-done | bytes 7340048 | tf_op jit(solution)/shard_map/all_gather | solution.py:53
  164.4 3.8 %convert_add_fusion = f32[8192,64]{1,0:T(8,128)S(1)} fusion(bf16[8192,448]{1,0:T(8,128)(2,1)} %all-gather.2.cloned.1.call-done), kind=kLoop, calls=%fused_computation.18 | loop fusion | flops 2621440 | bytes 5242880 | tf_op jit(solution)/shard_map/add | solution.py:64
  168.2 2.0 copy-done.1
  170.2 7.1 %fusion.42 = f32[64,64]{1,0:T(8,128)S(1)} fusion(f32[8192,64]{1,0:T(8,128)S(1)} %convert_add_fusion), kind=kOutput, calls=%fused_computation.99 | convolution fusion | flops 402653184 | bytes 2113536 | tf_op jit(solution)/shard_map/dot_general | solution.py:17
  177.4 5.8 %cholesky.74 = f32[64,64]{1,0:T(8,128)S(1)} custom-call(f32[64,64]{1,0:T(8,128)S(1)} %fusion.29), custom_call_target="Cholesky" | custom-call | tf_op jit(solution)/shard_map/jit(cholesky)/cholesky | solution.py:21
  184.6 4.9 %custom-call.10 = f32[1,64,64]{1,2,0:T(8,128)S(1)} custom-call(f32[1,64,64]{2,1,0:T(8,128)S(1)} %fusion.13), custom_call_target="InvertDiagBlocksLowerTriangular" | custom-call | tf_op jit(solution)/shard_map/triangular_solve/custom-call.0 | solution.py:22
  189.5 6.5 %convolution_bitcast_fusion.1 = f32[8192,64]{0,1:T(8,128)S(1)} fusion(f32[8192,64]{1,0:T(8,128)} %copy-done.1, f32[1,64,64]{1,2,0:T(8,128)S(1)} %custom-call.10), kind=kOutput, calls=%fused_computation.16 | convolution fusion | flops 402653184 | bytes 4210688 | tf_op jit(solution)/shard_map/triangular_solve/dot.16 | solution.py:22
  195.9 1.8 fusion.43
  197.8 5.8 %cholesky.85 = f32[64,64]{1,0:T(8,128)S(1)} custom-call(f32[64,64]{1,0:T(8,128)S(1)} %fusion.27), custom_call_target="Cholesky" | custom-call | tf_op jit(solution)/shard_map/jit(cholesky)/cholesky | solution.py:21
  205.0 4.9 %custom-call.11 = f32[1,64,64]{1,2,0:T(8,128)S(1)} custom-call(f32[1,64,64]{2,1,0:T(8,128)S(1)} %fusion.14), custom_call_target="InvertDiagBlocksLowerTriangular" | custom-call | tf_op jit(solution)/shard_map/triangular_solve/custom-call.0 | solution.py:22
  209.9 3.3 %fusion.41 = (bf16[8192,64]{0,1:T(8,128)(2,1)S(1)}, f32[8192,64]{0,1:T(8,128)}) fusion(f32[8192,64]{0,1:T(8,128)S(1)} %convolution_bitcast_fusion.1, f32[1,64,64]{1,2,0:T(8,128)S(1)} %custom-call.11), kind=kOutput, calls=%fused_computation.98 | convolution fusion | flops 403177472 | bytes 5259264 | tf_op jit(solution)/shard_map/triangular_solve/dot.16 | solution.py:22
  214.3 2.5 slice.59
  216.8 5.0 %convolution_bitcast_fusion.6 = f32[128,320]{0,1:T(8,128)S(1)} fusion(bf16[128,8192]{1,0:T(8,128)(2,1)} %collective-permute-done, bf16[8192,64]{1,0:T(8,128)(2,1)S(1)} %copy.67, bf16[8192,256]{1,0:T(8,128)(2,1)S(1)} %slice.59), kind=kOutput, calls=%fused_computation.24 | convolution fusion | flops 681574400 | bytes 7503872 | tf_op jit(solution)/shard_map/dot_general | solution.py:76
  222.5 4.7 %convolution_bitcast_fusion.5 = f32[128,320]{0,1:T(8,128)S(1)} fusion(bf16[128,8192]{1,0:T(8,128)(2,1)} %collective-permute-done.1, bf16[8192,64]{1,0:T(8,128)(2,1)S(1)} %copy.67, bf16[8192,256]{1,0:T(8,128)(2,1)} %copy-done.2), kind=kOutput, calls=%fused_computation.23 | convolution fusion | flops 681574400 | bytes 7503872 | tf_op jit(solution)/shard_map/dot_general | solution.py:76
  227.9 4.8 %convolution_bitcast_fusion.7 = f32[128,320]{0,1:T(8,128)S(1)} fusion(bf16[1,128,8192]{2,1,0:T(8,128)(2,1)} %param.14, bf16[8192,64]{1,0:T(8,128)(2,1)S(1)} %copy.67, bf16[8192,256]{1,0:T(8,128)(2,1)} %copy-done.2), kind=kOutput, calls=%fused_computation.25 | convolution fusion | flops 681574400 | bytes 7503872 | tf_op jit(solution)/shard_map/dot_general | solution.py:76
  232.7 3.4 %convolution_bitcast_fusion.4 = f32[128,320]{0,1:T(8,128)S(1)} fusion(bf16[128,8192]{1,0:T(8,128)(2,1)} %collective-permute-done.2, bf16[8192,64]{1,0:T(8,128)(2,1)S(1)} %copy.67, bf16[8192,256]{1,0:T(8,128)(2,1)S(1)} %copy-done.3), kind=kOutput, calls=%fused_computation.22 | convolution fusion | flops 681574400 | bytes 7503872 | tf_op jit(solution)/shard_map/dot_general | solution.py:76
  237.5 25.5 %while.23 = (s32[]{:T(128)}, f32[2,2]{1,0:T(2,128)S(1)}, bf16[2,8,512,128]{2,3,1,0:T(8,128)(2,1)}, bf16[2,2,512,128]{3,2,1,0:T(8,128)(2,1)S(1)}, s32[512]{0:T(51...) while((s32[]{:T(128)}, f32[2,2]{1,0:T(2,128)S(1)}, ...), condition=%wide.region_9.13_spmd.clone, body=%wide.region_2.12_spmd.clone.sunk | while | flops 138674192 | bytes 10115450 | solution.py:111
  239.8 10.4 %while.24 = (s32[]{:T(128)}, f32[8,2]{1,0:T(8,128)S(1)}, pred[512,512]{0,1:T(8,128)(4,1)S(1)}, bf16[8,512,128]{2,1,0:T(8,128)(2,1)S(1)}, bf16[2,512,128]{2,1,0:T(8,128)(2,1)S(1)}, /*index=5*/s32[]{:T(128)}, s32[]{:T(128)}) while((s32[]{:T(128)}, f32[8,2]{1,0:T(8,128)S(1)}, pred[512,512]{0,1:T(8,128)(4,1)S(1)}, ...), condition=%wide.region_7.10_spmd, body=%wide.region_3.0_spmd.sunk | while | flops 138412032 | bytes 5132397 | solution.py:108
  252.5 10.4 %while.24 = (s32[]{:T(128)}, f32[8,2]{1,0:T(8,128)S(1)}, pred[512,512]{0,1:T(8,128)(4,1)S(1)}, bf16[8,512,128]{2,1,0:T(8,128)(2,1)S(1)}, bf16[2,512,128]{2,1,0:T(8,128)(2,1)S(1)}, /*index=5*/s32[]{:T(128)}, s32[]{:T(128)}) while((s32[]{:T(128)}, f32[8,2]{1,0:T(8,128)S(1)}, pred[512,512]{0,1:T(8,128)(4,1)S(1)}, ...), condition=%wide.region_7.10_spmd, body=%wide.region_3.0_spmd.sunk | while | flops 138412032 | bytes 5132397 | solution.py:108
  263.7 9.6 %all-to-all-start = ((f32[128,1,2]{2,1,0:T(1,128)}), f32[128,1,2]{2,1,0:T(1,128)S(1)}, u32[]{:S(2)}, u32[]{:S(2)}) async-start(f32[128,1,2]{2,1,0:T(1,128)} %broadcast_in_dim.47), calls=%async_computation | async-start | bytes 131072 | tf_op jit(solution)/shard_map/all_to_all | solution.py:42
  273.3 1.9 convolution_multiply_fusion
  275.3 12.9 %all-to-all-done = f32[128,1,2]{2,1,0:T(1,128)S(1)} async-done(((f32[128,1,2]{2,1,0:T(1,128)}), f32[128,1,2]{2,1,0:T(1,128)S(1)}, u32[]{:S(2)}, u32[]{:S(2)}) %all-to-all-start) | async-done | bytes 1056 | tf_op jit(solution)/shard_map/all_to_all | solution.py:42
  288.3 7.9 %all_to_all.12 = f32[4,1,2]{2,1,0:T(1,128)S(1)} all-to-all(f32[4,1,2]{2,1,0:T(1,128)S(1)} %broadcast_in_dim.48), channel_id=1, replica_groups=mesh['fsdp'=128,'seq'=4] {'seq'}, dimensions={0} | all-to-all | bytes 64 | tf_op jit(solution)/shard_map/all_to_all | solution.py:42
  (142 shorter events, 39.1 us)
Async XLA Ops:
  7.2 13.9 %copy-start = (f32[1024,64]{0,1:T(8,128)S(1)}, f32[1024,64]{0,1:T(8,128)}, u32[]{:S(2)}) copy-start(f32[1024,64]{0,1:T(8,128)} %param.18) | copy-start | bytes 786436
  7.2 39.4 %copy-start.5 = (bf16[1,512,2048]{2,1,0:T(8,128)(2,1)S(1)}, bf16[1,512,2048]{2,1,0:T(8,128)(2,1)}, u32[]{:S(2)}) copy-start(bf16[1,512,2048]{2,1,0:T(8,128)(2,1)} %param.15) | copy-start | bytes 6291460
  7.2 157.2 %all-gather.2.cloned.1.call-start = ((), (), s32[]{:S(2)}) async-start(), calls=%async_computation.2 | async-start | bytes 8454144 | tf_op jit(solution)/shard_map/all_gather | solution.py:53
  9.7 207.1 %collective-permute-start = (bf16[128,8192]{1,0:T(8,128)(2,1)}, bf16[128,8192]{1,0:T(8,128)(2,1)}, u32[]{:S(2)}, u32[]{:S(2)}) collective-permute-start(bf16[128,8192]{1,0:T(8,128)(2,1)} %bitcast.137), channel_id=1, source_target_pairs={{0,1},{1,2},{2,3},{3,0},{4,5},{5,6},{6,7},{7,4},{8,9},{9,10},{10,1... | collective-permute-start | bytes 6291464 | tf_op jit(solution)/shard_map/ppermute | solution.py:59
  13.6 208.9 %collective-permute-start.1 = (bf16[128,8192]{1,0:T(8,128)(2,1)}, bf16[128,8192]{1,0:T(8,128)(2,1)}, u32[]{:S(2)}, u32[]{:S(2)}) collective-permute-start(bf16[128,8192]{1,0:T(8,128)(2,1)} %bitcast.138), channel_id=1, source_target_pairs={{0,2},{1,3},{2,0},{3,1},{4,6},{5,7},{6,4},{7,5},{8,10},{9,11},{10,... | collective-permute-start | bytes 6291464 | tf_op jit(solution)/shard_map/ppermute | solution.py:59
  18.0 214.7 %collective-permute-start.2 = (bf16[128,8192]{1,0:T(8,128)(2,1)}, bf16[128,8192]{1,0:T(8,128)(2,1)}, u32[]{:S(2)}, u32[]{:S(2)}) collective-permute-start(bf16[128,8192]{1,0:T(8,128)(2,1)} %bitcast.139), channel_id=1, source_target_pairs={{0,3},{1,0},{2,1},{3,2},{4,7},{5,4},{6,5},{7,6},{8,11},{9,8},{10,9... | collective-permute-start | bytes 6291464 | tf_op jit(solution)/shard_map/ppermute | solution.py:59
  168.2 2.0 copy-start.1
  216.7 5.1 %copy-start.2 = (bf16[8192,256]{1,0:T(8,128)(2,1)}, bf16[8192,256]{1,0:T(8,128)(2,1)S(1)}, u32[]{:S(2)}) copy-start(bf16[8192,256]{1,0:T(8,128)(2,1)S(1)} %slice.59) | copy-start | bytes 12582916
  216.8 5.1 %copy-start.4 = (f32[1024,64]{0,1:T(8,128)S(1)}, f32[1024,64]{0,1:T(8,128)}, u32[]{:S(2)}) copy-start(f32[1024,64]{0,1:T(8,128)} %convolution_bitcast_fusion.2) | copy-start | bytes 786436
  227.9 4.9 %copy-start.3 = (bf16[8192,256]{1,0:T(8,128)(2,1)S(1)}, bf16[8192,256]{1,0:T(8,128)(2,1)}, u32[]{:S(2)}) copy-start(bf16[8192,256]{1,0:T(8,128)(2,1)} %copy-done.2) | copy-start | bytes 12582916
  263.7 24.5 %all-to-all-start = ((f32[128,1,2]{2,1,0:T(1,128)}), f32[128,1,2]{2,1,0:T(1,128)S(1)}, u32[]{:S(2)}, u32[]{:S(2)}) async-start(f32[128,1,2]{2,1,0:T(1,128)} %broadcast_in_dim.47), calls=%async_computation | async-start | bytes 131072 | tf_op jit(solution)/shard_map/all_to_all | solution.py:42
Sparse Core Ops, SparseCore 0:
  11.1 153.2 all-gather.1

commit v3 on v2

--- a/solution.py
+++ b/solution.py
@@ -26,6 +26,19 @@
     for turn in range(2):
         factor = solve_rows(factor, highest(factor.T, factor))
     return factor
+
+
+def orthonormal_map(factor):
+    gram = highest(factor.T, factor)
+    eye = jnp.eye(gram.shape[0], dtype=gram.dtype)
+    first = lax.linalg.triangular_solve(
+        jnp.linalg.cholesky(gram), eye, left_side=False, lower=True, transpose_a=True
+    )
+    second_gram = highest(first.T, highest(gram, first))
+    second = lax.linalg.triangular_solve(
+        jnp.linalg.cholesky(second_gram), eye, left_side=False, lower=True, transpose_a=True
+    )
+    return highest(factor, highest(first, second))
 
 
 def split3(values):
@@ -65,20 +78,17 @@
         whole[:, slice_width : slice_width + r].astype(jnp.float32)
         + whole[:, slice_width + r : slice_width + 2 * r].astype(jnp.float32)
     ) + whole[:, slice_width + 2 * r :].astype(jnp.float32)
-    q_u = orthonormal(lax.optimization_barrier(u_whole))
+    q_u = orthonormal_map(lax.optimization_barrier(u_whole))
     q_low = q_u.astype(jnp.bfloat16)
     both = jnp.concatenate([weight_piece, q_low], axis=1)
 
     col_start = me_seq * slice_width
     v_slice = lax.dynamic_slice_in_dim(q_v, col_start, slice_width, 0)
-    key_parts = []
-    for part in chunks:
-        prod = jnp.dot(part, both, preferred_element_type=jnp.float32)
-        base = prod[:, :slice_width]
-        side = prod[:, slice_width:]
-        offset = 2.0 * highest(side, v_slice.T)
-        key_parts.append(jnp.stack([base + offset, base - offset]).astype(jnp.bfloat16))
-    keys = jnp.concatenate(key_parts, axis=1)
+    prod = jnp.dot(jnp.concatenate(chunks, axis=0), both, preferred_element_type=jnp.float32)
+    base = prod[:, :slice_width]
+    side = prod[:, slice_width:]
+    offset = 2.0 * highest(side, v_slice.T)
+    keys = jnp.stack([base + offset, base - offset]).astype(jnp.bfloat16)
     length = keys.shape[1]
 
     block = (me_seq - jnp.arange(n_seq)) % n_seq

time: 309 us -> 289 us (0.935); the launches traced: 304 us -> 289 us
  matrix products: 51.2 us -> 36.8 us
    another operation x3 -> x13, other arithmetic: 0.01 us -> 24.1 us  [the longest x3 6.52 us: orthonormal_map(): jnp.linalg.cholesky(second_gram)]
    another operation x12 -> x6, other arithmetic: 26.1 us -> 13 us  [solve_rows(): lower = jnp.linalg.cholesky(gram)]
    dot_general x4 -> x1, matrix products: 18 us -> 5.56 us  [local(): jnp.dot(jnp.concatenate(chunks, axis=0), both, preferred_element_type=jnp...]
    another operation x8 -> x4, other arithmetic: 22.2 us -> 11.1 us  [solve_rows(): lax.linalg.triangular_solve(lower, rows, left_side=False, lower=True, tra...]
    another operation x4 -> x2, matrix products: 11.3 us -> 1.53 us  [solve_rows(): lax.linalg.triangular_solve(lower, rows, left_side=False, lower=True, tra...]
    dot_general x9, matrix products: 13.2 us -> 20.4 us  [highest(): jnp.dot(left, right, precision=lax.Precision.HIGHEST, preferred_element_t...]
  transfers between devices with their start and end apart: 5 -> 5, of which waited for: 2 -> 2; matrix products, arithmetic and copies ran while one was open for 32% -> 27% of each run, Pallas kernels for 0% -> 0%
where the time goes in v3:
time: 289 us
  waiting for transfers between devices  127 us (44%)
  other arithmetic  67 us (23%)
  matrix products  36.8 us (13%)
  starting transfers between devices  21 us (7%)
  local copies, waits for them, and re-layouts  14.4 us (5%)
  between operations  14.4 us (5%)
  blocking collectives  7.89 us (3%)
    all_gather x1, waiting for transfers between devices, local(): whole = lax.all_gather(packed, 'fsdp', axis=0, tiled=True)  114 us
    dot_general x9, matrix products, highest(): jnp.dot(left, right, precision=lax.Precision.HIGHEST, preferred_element_t...  20.4 us
    another operation x6, other arithmetic, solve_rows(): lower = jnp.linalg.cholesky(gram)  13 us
    all_to_all x1, waiting for transfers between devices, total_over(): return jnp.sum(lax.all_to_all(spread, axis, 0, 0, tiled=True), axis=0)  12.9 us
    ppermute x3, starting transfers between devices, local(): lax.ppermute(x_local, 'seq', [(i, (i + shift) % n_seq) for i in range(n_s...  11.4 us
    another operation x4, other arithmetic, solve_rows(): lax.linalg.triangular_solve(lower, rows, left_side=False, lower=True, tra...  11.1 us
    all_to_all x1, starting transfers between devices, total_over(): return jnp.sum(lax.all_to_all(spread, axis, 0, 0, tiled=True), axis=0)  9.62 us
    reduce_sum x16, other arithmetic, one_query_head(): jnp.sum(jnp.where(causal[None], jnp.exp(scores - top[..., None]), 0.0), a...  9.15 us
  transfers between devices with their start and end apart: 5, of which 2 were waited for; matrix products, arithmetic and copies ran while one was open for 27% of the time, Pallas kernels for 0%

profile of v3, /device:TPU:1, one launch (start us, length us, event | category | flops | bytes accessed | tf_op | source)
XLA Modules:
  0.0 288.8 jit_solution(2902003976088465910)
XLA Ops:
  8.2 1.5 pad_maximum_fusion
  9.7 3.9 %collective-permute-start = (bf16[128,8192]{1,0:T(8,128)(2,1)}, bf16[128,8192]{1,0:T(8,128)(2,1)}, u32[]{:S(2)}, u32[]{:S(2)}) collective-permute-start(bf16[128,8192]{1,0:T(8,128)(2,1)} %bitcast.114), channel_id=1, source_target_pairs={{0,1},{1,2},{2,3},{3,0},{4,5},{5,6},{6,7},{7,4},{8,9},{9,10},{10,1... | collective-permute-start | bytes 6291464 | tf_op jit(solution)/shard_map/ppermute | solution.py:72
  13.6 4.4 %collective-permute-start.1 = (bf16[128,8192]{1,0:T(8,128)(2,1)}, bf16[128,8192]{1,0:T(8,128)(2,1)}, u32[]{:S(2)}, u32[]{:S(2)}) collective-permute-start(bf16[128,8192]{1,0:T(8,128)(2,1)} %bitcast.115), channel_id=1, source_target_pairs={{0,2},{1,3},{2,0},{3,1},{4,6},{5,7},{6,4},{7,5},{8,10},{9,11},{10,... | collective-permute-start | bytes 6291464 | tf_op jit(solution)/shard_map/ppermute | solution.py:72
  18.0 3.1 %collective-permute-start.2 = (bf16[128,8192]{1,0:T(8,128)(2,1)}, bf16[128,8192]{1,0:T(8,128)(2,1)}, u32[]{:S(2)}, u32[]{:S(2)}) collective-permute-start(bf16[128,8192]{1,0:T(8,128)(2,1)} %bitcast.116), channel_id=1, source_target_pairs={{0,3},{1,0},{2,1},{3,2},{4,7},{5,4},{6,5},{7,6},{8,11},{9,8},{10,9... | collective-permute-start | bytes 6291464 | tf_op jit(solution)/shard_map/ppermute | solution.py:72
  21.5 5.8 %cholesky.96 = f32[64,64]{1,0:T(8,128)S(1)} custom-call(f32[64,64]{1,0:T(8,128)S(1)} %fusion.32), custom_call_target="Cholesky" | custom-call | tf_op jit(solution)/shard_map/jit(cholesky)/cholesky | solution.py:21
  28.7 4.9 %custom-call.12 = f32[1,64,64]{1,2,0:T(8,128)S(1)} custom-call(f32[1,64,64]{2,1,0:T(8,128)S(1)} %fusion.26), custom_call_target="InvertDiagBlocksLowerTriangular" | custom-call | tf_op jit(solution)/shard_map/triangular_solve/custom-call.2 | solution.py:22
  34.5 5.9 %cholesky.107 = f32[64,64]{1,0:T(8,128)S(1)} custom-call(f32[64,64]{1,0:T(8,128)S(1)} %fusion.30), custom_call_target="Cholesky" | custom-call | tf_op jit(solution)/shard_map/jit(cholesky)/cholesky | solution.py:21
  41.7 4.9 %custom-call.13 = f32[1,64,64]{1,2,0:T(8,128)S(1)} custom-call(f32[1,64,64]{2,1,0:T(8,128)S(1)} %fusion.27), custom_call_target="InvertDiagBlocksLowerTriangular" | custom-call | tf_op jit(solution)/shard_map/triangular_solve/custom-call.2 | solution.py:22
  46.6 2.5 copy.36
  49.2 1.1 convolution_bitcast_fusion
  50.3 114.1 %all-gather.2.cloned.1.call-done = bf16[8192,448]{1,0:T(8,128)(2,1)} async-done(((bf16[64,448]{1,0:T(8,128)(2,1)}), bf16[8192,448]{1,0:T(8,128)(2,1)}) %all-gather.2.cloned.1.call-update) | async-done | bytes 7340048 | tf_op jit(solution)/shard_map/all_gather | solution.py:66
  164.4 3.8 %convert_add_fusion = f32[8192,64]{1,0:T(8,128)S(1)} fusion(bf16[8192,448]{1,0:T(8,128)(2,1)} %all-gather.2.cloned.1.call-done), kind=kLoop, calls=%fused_computation.26 | loop fusion | flops 2621440 | bytes 5242880 | tf_op jit(solution)/shard_map/add | solution.py:77
  168.2 2.0 copy-done.1
  170.2 7.1 %fusion.44 = f32[64,64]{1,0:T(8,128)S(1)} fusion(f32[8192,64]{1,0:T(8,128)S(1)} %convert_add_fusion), kind=kOutput, calls=%fused_computation.88 | convolution fusion | flops 402653184 | bytes 2113536 | tf_op jit(solution)/shard_map/dot_general | solution.py:17
  177.4 5.8 %cholesky.74 = f32[64,64]{1,0:T(8,128)S(1)} custom-call(f32[64,64]{1,0:T(8,128)S(1)} %fusion.36), custom_call_target="Cholesky" | custom-call | tf_op jit(solution)/shard_map/jit(cholesky)/cholesky | solution.py:35
  184.6 4.9 %custom-call.10 = f32[1,64,64]{1,2,0:T(8,128)S(1)} custom-call(f32[1,64,64]{2,1,0:T(8,128)S(1)} %fusion.24), custom_call_target="InvertDiagBlocksLowerTriangular" | custom-call | tf_op jit(solution)/shard_map/triangular_solve/custom-call.0 | solution.py:34
  190.2 5.8 %cholesky.85 = f32[64,64]{1,0:T(8,128)S(1)} custom-call(f32[64,64]{1,0:T(8,128)S(1)} %fusion.34), custom_call_target="Cholesky" | custom-call | tf_op jit(solution)/shard_map/jit(cholesky)/cholesky | solution.py:39
  197.4 4.9 %custom-call.11 = f32[1,64,64]{1,2,0:T(8,128)S(1)} custom-call(f32[1,64,64]{2,1,0:T(8,128)S(1)} %fusion.25), custom_call_target="InvertDiagBlocksLowerTriangular" | custom-call | tf_op jit(solution)/shard_map/triangular_solve/custom-call.0 | solution.py:38
  202.8 8.5 %fusion.43 = (bf16[8192,64]{0,1:T(8,128)(2,1)S(1)}, f32[8192,64]{0,1:T(8,128)}) fusion(f32[8192,64]{1,0:T(8,128)} %copy-done.1, f32[64,64]{1,0:T(8,128)S(1)} %fusion.47), kind=kOutput, calls=%fused_computation.87 | convolution fusion | flops 403177472 | bytes 5259264 | tf_op jit(solution)/shard_map/dot_general | solution.py:17
  211.3 1.1 copy.37
  212.4 2.1 slice-done
  215.3 5.6 %fusion.9 = f32[512,320]{0,1:T(8,128)S(1)} fusion(bf16[128,8192]{1,0:T(8,128)(2,1)} %collective-permute-done.2, bf16[128,8192]{1,0:T(8,128)(2,1)} %collective-permute-done.1, bf16[128,8192]{1,0:T(8,128)(2,1)} %collective-permute-done, bf16[128,8192]{1,0:T(8,128)(2,1)S(1)} %bitcast.117, bf16[8192,64]{1,0:T(8,128)(2,1)S(1)} %copy.37, ...), kind=kOutput, calls=%fused_computation.15 | convolution fusion | flops 2728394752 | bytes 14286848 | tf_op jit(solution)/shard_map/dot_general | solution.py:87
  220.8 1.5 add_convert_fusion
  222.8 25.5 %while.23 = (s32[]{:T(128)}, f32[2,2]{1,0:T(2,128)S(1)}, bf16[2,8,512,128]{2,3,1,0:T(8,128)(2,1)}, bf16[2,2,512,128]{3,2,1,0:T(8,128)(2,1)S(1)}, s32[512]{0:T(51...) while((s32[]{:T(128)}, f32[2,2]{1,0:T(2,128)S(1)}, ...), condition=%wide.region_9.13_spmd.clone, body=%wide.region_2.12_spmd.clone.sunk | while | flops 138674192 | bytes 10115450 | solution.py:121
  222.8 1.4 constant_dynamic-slice_fusion.2
  225.1 10.4 %while.24 = (s32[]{:T(128)}, f32[8,2]{1,0:T(8,128)S(1)}, pred[512,512]{0,1:T(8,128)(4,1)S(1)}, bf16[8,512,128]{2,1,0:T(8,128)(2,1)S(1)}, bf16[2,512,128]{2,1,0:T(8,128)(2,1)S(1)}, /*index=5*/s32[]{:T(128)}, s32[]{:T(128)}) while((s32[]{:T(128)}, f32[8,2]{1,0:T(8,128)S(1)}, pred[512,512]{0,1:T(8,128)(4,1)S(1)}, ...), condition=%wide.region_7.10_spmd, body=%wide.region_3.0_spmd.sunk | while | flops 138412032 | bytes 5132397 | solution.py:118
  235.5 1.3 constant_dynamic-slice_fusion.2
  237.8 10.4 %while.24 = (s32[]{:T(128)}, f32[8,2]{1,0:T(8,128)S(1)}, pred[512,512]{0,1:T(8,128)(4,1)S(1)}, bf16[8,512,128]{2,1,0:T(8,128)(2,1)S(1)}, bf16[2,512,128]{2,1,0:T(8,128)(2,1)S(1)}, /*index=5*/s32[]{:T(128)}, s32[]{:T(128)}) while((s32[]{:T(128)}, f32[8,2]{1,0:T(8,128)S(1)}, pred[512,512]{0,1:T(8,128)(4,1)S(1)}, ...), condition=%wide.region_7.10_spmd, body=%wide.region_3.0_spmd.sunk | while | flops 138412032 | bytes 5132397 | solution.py:118
  248.9 9.6 %all-to-all-start = ((f32[128,1,2]{2,1,0:T(1,128)}), f32[128,1,2]{2,1,0:T(1,128)S(1)}, u32[]{:S(2)}, u32[]{:S(2)}) async-start(f32[128,1,2]{2,1,0:T(1,128)} %broadcast_in_dim.47), calls=%async_computation | async-start | bytes 131072 | tf_op jit(solution)/shard_map/all_to_all | solution.py:55
  258.6 1.9 convolution_multiply_fusion.1
  260.5 12.9 %all-to-all-done = f32[128,1,2]{2,1,0:T(1,128)S(1)} async-done(((f32[128,1,2]{2,1,0:T(1,128)}), f32[128,1,2]{2,1,0:T(1,128)S(1)}, u32[]{:S(2)}, u32[]{:S(2)}) %all-to-all-start) | async-done | bytes 1056 | tf_op jit(solution)/shard_map/all_to_all | solution.py:55
  273.6 7.9 %all_to_all.12 = f32[4,1,2]{2,1,0:T(1,128)S(1)} all-to-all(f32[4,1,2]{2,1,0:T(1,128)S(1)} %broadcast_in_dim.48), channel_id=1, replica_groups=mesh['fsdp'=128,'seq'=4] {'seq'}, dimensions={0} | all-to-all | bytes 64 | tf_op jit(solution)/shard_map/all_to_all | solution.py:55
  (132 shorter events, 33.8 us)
Async XLA Ops:
  7.2 13.9 %copy-start = (f32[1024,64]{0,1:T(8,128)S(1)}, f32[1024,64]{0,1:T(8,128)}, u32[]{:S(2)}) copy-start(f32[1024,64]{0,1:T(8,128)} %param.18) | copy-start | bytes 786436
  7.2 39.4 %copy-start.2 = (bf16[1,512,2048]{2,1,0:T(8,128)(2,1)S(1)}, bf16[1,512,2048]{2,1,0:T(8,128)(2,1)}, u32[]{:S(2)}) copy-start(bf16[1,512,2048]{2,1,0:T(8,128)(2,1)} %param.15) | copy-start | bytes 6291460
  7.2 157.3 %all-gather.2.cloned.1.call-start = ((), (), s32[]{:S(2)}) async-start(), calls=%async_computation.2 | async-start | bytes 8454144 | tf_op jit(solution)/shard_map/all_gather | solution.py:66
  9.7 202.8 %collective-permute-start = (bf16[128,8192]{1,0:T(8,128)(2,1)}, bf16[128,8192]{1,0:T(8,128)(2,1)}, u32[]{:S(2)}, u32[]{:S(2)}) collective-permute-start(bf16[128,8192]{1,0:T(8,128)(2,1)} %bitcast.114), channel_id=1, source_target_pairs={{0,1},{1,2},{2,3},{3,0},{4,5},{5,6},{6,7},{7,4},{8,9},{9,10},{10,1... | collective-permute-start | bytes 6291464 | tf_op jit(solution)/shard_map/ppermute | solution.py:72
  13.6 198.8 %collective-permute-start.1 = (bf16[128,8192]{1,0:T(8,128)(2,1)}, bf16[128,8192]{1,0:T(8,128)(2,1)}, u32[]{:S(2)}, u32[]{:S(2)}) collective-permute-start(bf16[128,8192]{1,0:T(8,128)(2,1)} %bitcast.115), channel_id=1, source_target_pairs={{0,2},{1,3},{2,0},{3,1},{4,6},{5,7},{6,4},{7,5},{8,10},{9,11},{10,... | collective-permute-start | bytes 6291464 | tf_op jit(solution)/shard_map/ppermute | solution.py:72
  18.0 194.5 %collective-permute-start.2 = (bf16[128,8192]{1,0:T(8,128)(2,1)}, bf16[128,8192]{1,0:T(8,128)(2,1)}, u32[]{:S(2)}, u32[]{:S(2)}) collective-permute-start(bf16[128,8192]{1,0:T(8,128)(2,1)} %bitcast.116), channel_id=1, source_target_pairs={{0,3},{1,0},{2,1},{3,2},{4,7},{5,4},{6,5},{7,6},{8,11},{9,8},{10,9... | collective-permute-start | bytes 6291464 | tf_op jit(solution)/shard_map/ppermute | solution.py:72
  168.2 2.0 copy-start.1
  212.4 2.2 slice-start
  212.4 2.9 copy-start.4
  222.7 35.8 %copy-start.3 = (f32[1024,64]{0,1:T(8,128)S(1)}, f32[1024,64]{0,1:T(8,128)}, u32[]{:S(2)}) copy-start(f32[1024,64]{0,1:T(8,128)} %convolution_bitcast_fusion) | copy-start | bytes 786436
  248.9 24.5 %all-to-all-start = ((f32[128,1,2]{2,1,0:T(1,128)}), f32[128,1,2]{2,1,0:T(1,128)S(1)}, u32[]{:S(2)}, u32[]{:S(2)}) async-start(f32[128,1,2]{2,1,0:T(1,128)} %broadcast_in_dim.47), calls=%async_computation | async-start | bytes 131072 | tf_op jit(solution)/shard_map/all_to_all | solution.py:55
Sparse Core Ops, SparseCore 0:
  11.1 153.2 all-gather.1

commit v4 on v3

--- a/solution.py
+++ b/solution.py
@@ -3,7 +3,9 @@
 import jax
 import jax.numpy as jnp
 from jax import lax
+from jax.experimental import pallas as pl
 from jax.sharding import PartitionSpec as P
+import functools
 
 D = 8192
 HQ = 64
@@ -39,6 +41,50 @@
         jnp.linalg.cholesky(second_gram), eye, left_side=False, lower=True, transpose_a=True
     )
     return highest(factor, highest(first, second))
+
+
+def lse_kernel(q_ref, k_ref, o_ref, *, blk, n_blk, scale):
+    for p in range(2):
+        for qb in range(n_blk):
+            q_blk = q_ref[qb * blk:(qb + 1) * blk, :]
+            m = None
+            l = None
+            for kb in range(qb + 1):
+                k_blk = k_ref[p, kb * blk:(kb + 1) * blk, :]
+                s = lax.dot_general(k_blk, q_blk, (((1,), (1,)), ((), ())),
+                                    preferred_element_type=jnp.float32) * scale
+                if kb == qb:
+                    rows = lax.broadcasted_iota(jnp.int32, s.shape, 0)
+                    cols = lax.broadcasted_iota(jnp.int32, s.shape, 1)
+                    s = jnp.where(rows <= cols, s, -1e30)
+                top = jnp.max(s, axis=0, keepdims=True)
+                if m is None:
+                    m = top
+                    l = jnp.sum(jnp.exp(s - m), axis=0, keepdims=True)
+                else:
+                    m_new = jnp.maximum(m, top)
+                    l = l * jnp.exp(m - m_new) + jnp.sum(jnp.exp(s - m_new), axis=0, keepdims=True)
+                    m = m_new
+            o_ref[0, p:p + 1, qb * blk:(qb + 1) * blk] = m + jnp.log(l)
+
+
+def lse_rows(query_rows, keys_nat, interpret=False):
+    length = query_rows.shape[0]
+    heads = query_rows.shape[1] // HD
+    kv = keys_nat.shape[2] // HD
+    blk = 128
+    kern = functools.partial(lse_kernel, blk=blk, n_blk=length // blk, scale=1.0 / math.sqrt(HD))
+    return pl.pallas_call(
+        kern,
+        grid=(kv, GROUP),
+        in_specs=[
+            pl.BlockSpec((length, HD), lambda k, g: (0, k * GROUP + g)),
+            pl.BlockSpec((2, length, HD), lambda k, g: (0, 0, k)),
+        ],
+        out_specs=pl.BlockSpec((1, 2, length), lambda k, g: (k * GROUP + g, 0, 0)),
+        out_shape=jax.ShapeDtypeStruct((heads, 2, length), jnp.float32),
+        interpret=interpret,
+    )(query_rows, keys_nat)
 
 
 def split3(values):
@@ -91,34 +137,11 @@
     keys = jnp.stack([base + offset, base - offset]).astype(jnp.bfloat16)
     length = keys.shape[1]
 
-    block = (me_seq - jnp.arange(n_seq)) % n_seq
-    key_pos = (block[:, None] * chunk + jnp.arange(chunk)[None, :]).reshape(length)
-
-    local_kv = slice_width // HD
-    query_rows = queries[0]
-    query_heads = query_rows.reshape(length, local_kv, GROUP, HD).transpose(1, 2, 0, 3)
-    key_heads = keys.reshape(2, length, local_kv, HD).transpose(2, 0, 1, 3)
-    places = jnp.arange(length)
-    causal = places[:, None] >= key_pos[None, :]
-    factor_scale = 1.0 / math.sqrt(HD)
-
-    def one_query_head(query_one, key_one):
-        scores = (
-            jnp.einsum("td,npd->ntp", query_one, key_one, preferred_element_type=jnp.float32)
-            * factor_scale
-        )
-        scores = jnp.where(causal[None], scores, -1e30)
-        top = jnp.max(scores, axis=-1)
-        total = jnp.sum(jnp.where(causal[None], jnp.exp(scores - top[..., None]), 0.0), axis=-1)
-        return jnp.sum(top + jnp.log(total), axis=1)
-
-    def one_key_head(pair):
-        group_queries, key_one = pair
-        return jnp.sum(
-            lax.map(lambda query_one: one_query_head(query_one, key_one), group_queries), axis=0
-        )
-
-    partial_sums = jnp.sum(lax.map(one_key_head, (query_heads, key_heads)), axis=0)
+    backwards = jnp.concatenate([keys[:, (n_seq - 1 - j) * chunk : (n_seq - j) * chunk] for j in range(n_seq)], axis=1)
+    doubled = jnp.concatenate([backwards, backwards], axis=1)
+    start = ((n_seq - 1 - me_seq) % n_seq) * chunk
+    keys_nat = lax.dynamic_slice_in_dim(doubled, start, length, 1)
+    partial_sums = jnp.sum(lse_rows(queries[0], keys_nat), axis=(0, 2))
     sums = total_over(total_over(partial_sums, "fsdp"), "seq")
     losses = sums / (lax.axis_size("fsdp") * length * HQ)
     unit = math.sqrt(D * KD / R)

time: 289 us -> 281 us (0.972)
  Pallas kernels: 0 us -> 14.1 us
  matrix products: 36.8 us -> 25.4 us
  other arithmetic: 67 us -> 56.3 us
  local copies, waits for them, and re-layouts: 14.4 us -> 10.1 us
  waiting for transfers between devices: 127 us -> 130 us
    pallas_call x0 -> x1, Pallas kernels: none -> 14.1 us  [lse_rows(): pl.pallas_call(kern, grid=(kv, GROUP), in_specs=[pl.BlockSpec((length, HD...]
    reduce_sum x35 -> x1, other arithmetic: 11.2 us -> 1.02 us  [local(): partial_sums = jnp.sum(lse_rows(queries[0], keys_nat), axis=(0, 2))]
    dot_general x16 -> x0, matrix products: 8.8 us -> none  [one_query_head(): jnp.einsum('td,npd->ntp', query_one, key_one, preferred_element_type=jnp....]
    dynamic_slice x4 -> x1, local copies, waits for them, and re-layouts: 4.02 us -> 0.83 us  [local(): keys_nat = lax.dynamic_slice_in_dim(doubled, start, length, 1)]
  transfers between devices with their start and end apart: 5 -> 5, of which waited for: 2 -> 2; matrix products, arithmetic and copies ran while one was open for 27% -> 26% of each run, Pallas kernels for 0% -> 0%
where the time goes in v4:
time: 281 us; the launch traced here: 280 us
  waiting for transfers between devices  130 us (46%)
  other arithmetic  56.3 us (20%)
  matrix products  25.4 us (9%)
  starting transfers between devices  21 us (7%)
  between operations  14.4 us (5%)
  Pallas kernels  14.1 us (5%)
  local copies, waits for them, and re-layouts  10.1 us (4%)
  blocking collectives  7.89 us (3%)
    all_gather x1, waiting for transfers between devices, local(): whole = lax.all_gather(packed, 'fsdp', axis=0, tiled=True)  117 us
    dot_general x9, matrix products, highest(): jnp.dot(left, right, precision=lax.Precision.HIGHEST, preferred_element_t...  17.8 us
    pallas_call x1, Pallas kernels, lse_rows(): pl.pallas_call(kern, grid=(kv, GROUP), in_specs=[pl.BlockSpec((length, HD...  14.1 us
    all_to_all x1, waiting for transfers between devices, total_over(): return jnp.sum(lax.all_to_all(spread, axis, 0, 0, tiled=True), axis=0)  13.7 us
    another operation x6, other arithmetic, solve_rows(): lower = jnp.linalg.cholesky(gram)  13 us
    ppermute x3, starting transfers between devices, local(): lax.ppermute(x_local, 'seq', [(i, (i + shift) % n_seq) for i in range(n_s...  11.4 us
    another operation x4, other arithmetic, solve_rows(): lax.linalg.triangular_solve(lower, rows, left_side=False, lower=True, tra...  11.1 us
    all_to_all x1, starting transfers between devices, total_over(): return jnp.sum(lax.all_to_all(spread, axis, 0, 0, tiled=True), axis=0)  9.62 us
  transfers between devices with their start and end apart: 5, of which 2 were waited for; matrix products, arithmetic and copies ran while one was open for 26% of the time, Pallas kernels for 0%

profile of v4, /device:TPU:1, one launch (start us, length us, event | category | flops | bytes accessed | tf_op | source)
XLA Modules:
  0.0 279.8 jit_solution(9005164947134443719)
XLA Ops:
  7.2 0.8 reduce-precision_convert_fusion.1
  8.0 1.5 pad_maximum_fusion.1
  9.5 3.9 %collective-permute-start = (bf16[128,8192]{1,0:T(8,128)(2,1)}, bf16[128,8192]{1,0:T(8,128)(2,1)}, u32[]{:S(2)}, u32[]{:S(2)}) collective-permute-start(bf16[128,8192]{1,0:T(8,128)(2,1)} %bitcast.68), channel_id=1, source_target_pairs={{0,1},{1,2},{2,3},{3,0},{4,5},{5,6},{6,7},{7,4},{8,9},{9,10},{10,1... | collective-permute-start | bytes 6291464 | tf_op jit(solution)/shard_map/ppermute | solution.py:118
  13.5 4.4 %collective-permute-start.1 = (bf16[128,8192]{1,0:T(8,128)(2,1)}, bf16[128,8192]{1,0:T(8,128)(2,1)}, u32[]{:S(2)}, u32[]{:S(2)}) collective-permute-start(bf16[128,8192]{1,0:T(8,128)(2,1)} %bitcast.69), channel_id=1, source_target_pairs={{0,2},{1,3},{2,0},{3,1},{4,6},{5,7},{6,4},{7,5},{8,10},{9,11},{10,... | collective-permute-start | bytes 6291464 | tf_op jit(solution)/shard_map/ppermute | solution.py:118
  17.9 3.1 %collective-permute-start.2 = (bf16[128,8192]{1,0:T(8,128)(2,1)}, bf16[128,8192]{1,0:T(8,128)(2,1)}, u32[]{:S(2)}, u32[]{:S(2)}) collective-permute-start(bf16[128,8192]{1,0:T(8,128)(2,1)} %bitcast.70), channel_id=1, source_target_pairs={{0,3},{1,0},{2,1},{3,2},{4,7},{5,4},{6,5},{7,6},{8,11},{9,8},{10,9... | collective-permute-start | bytes 6291464 | tf_op jit(solution)/shard_map/ppermute | solution.py:118
  21.4 5.8 %cholesky.96 = f32[64,64]{1,0:T(8,128)S(1)} custom-call(f32[64,64]{1,0:T(8,128)S(1)} %fusion.28), custom_call_target="Cholesky" | custom-call | tf_op jit(solution)/shard_map/jit(cholesky)/cholesky | solution.py:23
  28.6 4.9 %custom-call.12 = f32[1,64,64]{1,2,0:T(8,128)S(1)} custom-call(f32[1,64,64]{2,1,0:T(8,128)S(1)} %fusion.22), custom_call_target="InvertDiagBlocksLowerTriangular" | custom-call | tf_op jit(solution)/shard_map/triangular_solve/custom-call.2 | solution.py:24
  34.4 5.9 %cholesky.107 = f32[64,64]{1,0:T(8,128)S(1)} custom-call(f32[64,64]{1,0:T(8,128)S(1)} %fusion.26), custom_call_target="Cholesky" | custom-call | tf_op jit(solution)/shard_map/jit(cholesky)/cholesky | solution.py:23
  41.6 4.9 %custom-call.13 = f32[1,64,64]{1,2,0:T(8,128)S(1)} custom-call(f32[1,64,64]{2,1,0:T(8,128)S(1)} %fusion.23), custom_call_target="InvertDiagBlocksLowerTriangular" | custom-call | tf_op jit(solution)/shard_map/triangular_solve/custom-call.2 | solution.py:24
  46.5 1.1 convolution_bitcast_fusion
  47.6 116.8 %all-gather.2.cloned.1.call-done = bf16[8192,448]{1,0:T(8,128)(2,1)} async-done(((bf16[64,448]{1,0:T(8,128)(2,1)}), bf16[8192,448]{1,0:T(8,128)(2,1)}) %all-gather.2.cloned.1.call-update) | async-done | bytes 7340048 | tf_op jit(solution)/shard_map/all_gather | solution.py:112
  164.4 3.8 %convert_add_fusion = f32[8192,64]{1,0:T(8,128)S(1)} fusion(bf16[8192,448]{1,0:T(8,128)(2,1)} %all-gather.2.cloned.1.call-done), kind=kLoop, calls=%fused_computation.11 | loop fusion | flops 2621440 | bytes 5242880 | tf_op jit(solution)/shard_map/add | solution.py:123
  168.2 2.0 copy-done.1
  170.2 7.3 %fusion.38 = f32[64,64]{1,0:T(8,128)S(1)} fusion(f32[8192,64]{1,0:T(8,128)S(1)} %convert_add_fusion), kind=kOutput, calls=%fused_computation.87 | convolution fusion | flops 402653184 | bytes 2113536 | tf_op jit(solution)/shard_map/dot_general | solution.py:19
  177.5 5.8 %cholesky.74 = f32[64,64]{1,0:T(8,128)S(1)} custom-call(f32[64,64]{1,0:T(8,128)S(1)} %fusion.32), custom_call_target="Cholesky" | custom-call | tf_op jit(solution)/shard_map/jit(cholesky)/cholesky | solution.py:37
  184.7 4.9 %custom-call.10 = f32[1,64,64]{1,2,0:T(8,128)S(1)} custom-call(f32[1,64,64]{2,1,0:T(8,128)S(1)} %fusion.20), custom_call_target="InvertDiagBlocksLowerTriangular" | custom-call | tf_op jit(solution)/shard_map/triangular_solve/custom-call.0 | solution.py:36
  190.3 5.8 %cholesky.85 = f32[64,64]{1,0:T(8,128)S(1)} custom-call(f32[64,64]{1,0:T(8,128)S(1)} %fusion.30), custom_call_target="Cholesky" | custom-call | tf_op jit(solution)/shard_map/jit(cholesky)/cholesky | solution.py:41
  197.5 4.9 %custom-call.11 = f32[1,64,64]{1,2,0:T(8,128)S(1)} custom-call(f32[1,64,64]{2,1,0:T(8,128)S(1)} %fusion.21), custom_call_target="InvertDiagBlocksLowerTriangular" | custom-call | tf_op jit(solution)/shard_map/triangular_solve/custom-call.0 | solution.py:40
  202.9 6.5 %fusion.37 = (bf16[8192,64]{0,1:T(8,128)(2,1)S(1)}, f32[8192,64]{0,1:T(8,128)S(1)}) fusion(f32[8192,64]{1,0:T(8,128)} %copy-done.1, f32[64,64]{1,0:T(8,128)S(1)} %fusion.41), kind=kOutput, calls=%fused_computation.86 | convolution fusion | flops 403177472 | bytes 5259264 | tf_op jit(solution)/shard_map/dot_general | solution.py:19
  209.5 1.8 copy.23
  211.3 2.2 slice-done
  213.5 0.7 copy-done.2
  214.8 5.6 %fusion = f32[512,320]{0,1:T(8,128)S(1)} fusion(bf16[128,8192]{1,0:T(8,128)(2,1)} %collective-permute-done.2, bf16[128,8192]{1,0:T(8,128)(2,1)} %collective-permute-done.1, bf16[128,8192]{1,0:T(8,128)(2,1)} %collective-permute-done, bf16[128,8192]{1,0:T(8,128)(2,1)S(1)} %bitcast.71, bf16[8192,64]{1,0:T(8,128)(2,1)S(1)} %copy-done.2, ...), kind=kOutput, calls=%fused_computation | convolution fusion | flops 2728394752 | bytes 14286848 | tf_op jit(solution)/shard_map/dot_general | solution.py:133
  220.3 0.8 copy-done.4
  221.4 1.5 convolution_multiply_fusion
  223.2 0.8 constant_dynamic-slice_fusion.k_ref
  224.1 14.1 %shard_map.68 = f32[16,2,512]{2,1,0:T(2,128)} custom-call(bf16[512,2048]{1,0:T(8,128)(2,1)} %bitcast.67, bf16[2,512,256]{2,1,0:T(8,128)(2,1)} %constant_dynamic-slice_fusion.k_ref), custom_call_target="tpu_custom_call" | custom-call | tf_op jit(solution)/shard_map/pallas_call | solution.py:77
  238.2 1.0 reduce_sum.27
  239.9 9.6 %all-to-all-start = ((f32[128,1,2]{2,1,0:T(1,128)}), f32[128,1,2]{2,1,0:T(1,128)S(1)}, u32[]{:S(2)}, u32[]{:S(2)}) async-start(f32[128,1,2]{2,1,0:T(1,128)} %broadcast_in_dim.5), calls=%async_computation | async-start | bytes 131072 | tf_op jit(solution)/shard_map/all_to_all | solution.py:101
  249.5 1.2 convolution_multiply_fusion.1
  250.7 13.7 %all-to-all-done = f32[128,1,2]{2,1,0:T(1,128)S(1)} async-done(((f32[128,1,2]{2,1,0:T(1,128)}), f32[128,1,2]{2,1,0:T(1,128)S(1)}, u32[]{:S(2)}, u32[]{:S(2)}) %all-to-all-start) | async-done | bytes 1056 | tf_op jit(solution)/shard_map/all_to_all | solution.py:101
  264.5 7.9 %all_to_all.12 = f32[4,1,2]{2,1,0:T(1,128)S(1)} all-to-all(f32[4,1,2]{2,1,0:T(1,128)S(1)} %broadcast_in_dim.6), channel_id=1, replica_groups=mesh['fsdp'=128,'seq'=4] {'seq'}, dimensions={0} | all-to-all | bytes 64 | tf_op jit(solution)/shard_map/all_to_all | solution.py:101
  (59 shorter events, 10.3 us)
Async XLA Ops:
  7.2 13.8 %copy-start = (f32[1024,64]{0,1:T(8,128)S(1)}, f32[1024,64]{0,1:T(8,128)}, u32[]{:S(2)}) copy-start(f32[1024,64]{0,1:T(8,128)} %param.14) | copy-start | bytes 786436
  7.2 157.2 %all-gather.2.cloned.1.call-start = ((), (), s32[]{:S(2)}) async-start(), calls=%async_computation.2 | async-start | bytes 8454144 | tf_op jit(solution)/shard_map/all_gather | solution.py:112
  9.5 201.8 %collective-permute-start = (bf16[128,8192]{1,0:T(8,128)(2,1)}, bf16[128,8192]{1,0:T(8,128)(2,1)}, u32[]{:S(2)}, u32[]{:S(2)}) collective-permute-start(bf16[128,8192]{1,0:T(8,128)(2,1)} %bitcast.68), channel_id=1, source_target_pairs={{0,1},{1,2},{2,3},{3,0},{4,5},{5,6},{6,7},{7,4},{8,9},{9,10},{10,1... | collective-permute-start | bytes 6291464 | tf_op jit(solution)/shard_map/ppermute | solution.py:118
  13.5 197.8 %collective-permute-start.1 = (bf16[128,8192]{1,0:T(8,128)(2,1)}, bf16[128,8192]{1,0:T(8,128)(2,1)}, u32[]{:S(2)}, u32[]{:S(2)}) collective-permute-start(bf16[128,8192]{1,0:T(8,128)(2,1)} %bitcast.69), channel_id=1, source_target_pairs={{0,2},{1,3},{2,0},{3,1},{4,6},{5,7},{6,4},{7,5},{8,10},{9,11},{10,... | collective-permute-start | bytes 6291464 | tf_op jit(solution)/shard_map/ppermute | solution.py:118
  17.9 193.5 %collective-permute-start.2 = (bf16[128,8192]{1,0:T(8,128)(2,1)}, bf16[128,8192]{1,0:T(8,128)(2,1)}, u32[]{:S(2)}, u32[]{:S(2)}) collective-permute-start(bf16[128,8192]{1,0:T(8,128)(2,1)} %bitcast.70), channel_id=1, source_target_pairs={{0,3},{1,0},{2,1},{3,2},{4,7},{5,4},{6,5},{7,6},{8,11},{9,8},{10,9... | collective-permute-start | bytes 6291464 | tf_op jit(solution)/shard_map/ppermute | solution.py:118
  168.2 2.0 copy-start.1
  211.3 2.2 slice-start
  211.3 2.9 %copy-start.2 = (bf16[8192,64]{1,0:T(8,128)(2,1)S(1)}, bf16[8192,64]{1,0:T(8,128)(2,1)}, u32[]{:S(2)}) copy-start(bf16[8192,64]{1,0:T(8,128)(2,1)} %copy.23) | copy-start | bytes 3145732
  211.3 3.5 %copy-start.5 = (bf16[1,128,8192]{2,1,0:T(8,128)(2,1)S(1)}, bf16[1,128,8192]{2,1,0:T(8,128)(2,1)}, u32[]{:S(2)}) copy-start(bf16[1,128,8192]{2,1,0:T(8,128)(2,1)} %param.10) | copy-start | bytes 6291460
  220.3 0.8 copy-start.4
  223.1 26.4 %copy-start.3 = (f32[1024,64]{0,1:T(8,128)S(1)}, f32[1024,64]{0,1:T(8,128)}, u32[]{:S(2)}) copy-start(f32[1024,64]{0,1:T(8,128)} %convolution_bitcast_fusion) | copy-start | bytes 786436
  239.9 24.5 %all-to-all-start = ((f32[128,1,2]{2,1,0:T(1,128)}), f32[128,1,2]{2,1,0:T(1,128)S(1)}, u32[]{:S(2)}, u32[]{:S(2)}) async-start(f32[128,1,2]{2,1,0:T(1,128)} %broadcast_in_dim.5), calls=%async_computation | async-start | bytes 131072 | tf_op jit(solution)/shard_map/all_to_all | solution.py:101
Sparse Core Ops, SparseCore 0:
  11.1 153.2 all-gather.1

commit v5 on v4

--- a/solution.py
+++ b/solution.py
@@ -87,6 +87,43 @@
     )(query_rows, keys_nat)
 
 
+def map_from_gram(gram):
+    eye = jnp.eye(gram.shape[0], dtype=gram.dtype)
+    first = lax.linalg.triangular_solve(
+        jnp.linalg.cholesky(gram), eye, left_side=False, lower=True, transpose_a=True
+    )
+    second_gram = highest(first.T, highest(gram, first))
+    second = lax.linalg.triangular_solve(
+        jnp.linalg.cholesky(second_gram), eye, left_side=False, lower=True, transpose_a=True
+    )
+    return highest(first, second)
+
+
+def gram_of_pieces(pieces, r):
+    full = lax.dot_general(pieces, pieces, (((0,), (0,)), ((), ())), preferred_element_type=jnp.float32)
+    block = lambda a, b: full[a * r : (a + 1) * r, b * r : (b + 1) * r]
+    order = [(2, 2), (2, 1), (1, 2), (1, 1), (0, 2), (2, 0), (0, 1), (1, 0), (0, 0)]
+    total = block(*order[0])
+    for a, b in order[1:]:
+        total = total + block(a, b)
+    return total
+
+
+def apply_to_pieces(pieces, mapping, r):
+    mh, mm, ml = split3(mapping)
+    zero = jnp.zeros_like(mh)
+    stack = jnp.concatenate(
+        [
+            jnp.concatenate([mh, mm, ml], axis=1),
+            jnp.concatenate([mh, mm, zero], axis=1),
+            jnp.concatenate([mh, zero, zero], axis=1),
+        ],
+        axis=0,
+    )
+    out = jnp.dot(pieces, stack, preferred_element_type=jnp.float32)
+    return (out[:, 2 * r :] + out[:, r : 2 * r]) + out[:, :r]
+
+
 def split3(values):
     hi = lax.reduce_precision(values, exponent_bits=8, mantissa_bits=7)
     rest = values - hi
@@ -120,11 +157,8 @@
     q_v = orthonormal(v_factor)
     weight_piece = whole[:, :slice_width]
     r = u_factor.shape[1]
-    u_whole = (
-        whole[:, slice_width : slice_width + r].astype(jnp.float32)
-        + whole[:, slice_width + r : slice_width + 2 * r].astype(jnp.float32)
-    ) + whole[:, slice_width + 2 * r :].astype(jnp.float32)
-    q_u = orthonormal_map(lax.optimization_barrier(u_whole))
+    pieces = whole[:, slice_width:]
+    q_u = apply_to_pieces(pieces, map_from_gram(gram_of_pieces(pieces, r)), r)
     q_low = q_u.astype(jnp.bfloat16)
     both = jnp.concatenate([weight_piece, q_low], axis=1)
 

time: 281 us -> 271 us (0.964)
  matrix products: 25.4 us -> 20.5 us
  other arithmetic: 56.3 us -> 53 us
    dot_general x9 -> x7, matrix products: 17.8 us -> 4.07 us  [highest(): jnp.dot(left, right, precision=lax.Precision.HIGHEST, preferred_element_t...]
    dot_general x0 -> x2, matrix products: none -> 8.82 us  [the longest x1 5 us: gram_of_pieces(): lax.dot_general(pieces, pieces, (((0,), (0,)), ((), ())), preferred_eleme...]
    add x1, other arithmetic: 3.79 us -> 0.09 us  [gram_of_pieces(): total = total + block(a, b)]
  transfers between devices with their start and end apart: 5 -> 5, of which waited for: 2 -> 2; matrix products, arithmetic and copies ran while one was open for 26% -> 24% of each run, Pallas kernels for 0% -> 0%
where the time goes in v5:
time: 271 us; the launch traced here: 270 us
  waiting for transfers between devices  130 us (48%)
  other arithmetic  53 us (20%)
  starting transfers between devices  21 us (8%)
  matrix products  20.5 us (8%)
  between operations  14.4 us (5%)
  Pallas kernels  14.1 us (5%)
  local copies, waits for them, and re-layouts  8.3 us (3%)
  blocking collectives  7.89 us (3%)
    all_gather x1, waiting for transfers between devices, local(): whole = lax.all_gather(packed, 'fsdp', axis=0, tiled=True)  117 us
    pallas_call x1, Pallas kernels, lse_rows(): pl.pallas_call(kern, grid=(kv, GROUP), in_specs=[pl.BlockSpec((length, HD...  14.1 us
    all_to_all x1, waiting for transfers between devices, total_over(): return jnp.sum(lax.all_to_all(spread, axis, 0, 0, tiled=True), axis=0)  13.7 us
    another operation x6, other arithmetic, solve_rows(): lower = jnp.linalg.cholesky(gram)  13 us
    ppermute x3, starting transfers between devices, local(): lax.ppermute(x_local, 'seq', [(i, (i + shift) % n_seq) for i in range(n_s...  11.4 us
    another operation x4, other arithmetic, solve_rows(): lax.linalg.triangular_solve(lower, rows, left_side=False, lower=True, tra...  11.1 us
    all_to_all x1, starting transfers between devices, total_over(): return jnp.sum(lax.all_to_all(spread, axis, 0, 0, tiled=True), axis=0)  9.62 us
    all_to_all x1, blocking collectives, total_over(): return jnp.sum(lax.all_to_all(spread, axis, 0, 0, tiled=True), axis=0)  7.89 us
  transfers between devices with their start and end apart: 5, of which 2 were waited for; matrix products, arithmetic and copies ran while one was open for 24% of the time, Pallas kernels for 0%

profile of v5, /device:TPU:1, one launch (start us, length us, event | category | flops | bytes accessed | tf_op | source)
XLA Modules:
  0.0 269.8 jit_solution(14239384472604423539)
XLA Ops:
  7.2 0.8 reduce-precision_convert_fusion.3
  8.0 1.5 pad_maximum_fusion.1
  9.5 3.9 %collective-permute-start = (bf16[128,8192]{1,0:T(8,128)(2,1)}, bf16[128,8192]{1,0:T(8,128)(2,1)}, u32[]{:S(2)}, u32[]{:S(2)}) collective-permute-start(bf16[128,8192]{1,0:T(8,128)(2,1)} %bitcast.64), channel_id=1, source_target_pairs={{0,1},{1,2},{2,3},{3,0},{4,5},{5,6},{6,7},{7,4},{8,9},{9,10},{10,1... | collective-permute-start | bytes 6291464 | tf_op jit(solution)/shard_map/ppermute | solution.py:155
  13.5 4.4 %collective-permute-start.1 = (bf16[128,8192]{1,0:T(8,128)(2,1)}, bf16[128,8192]{1,0:T(8,128)(2,1)}, u32[]{:S(2)}, u32[]{:S(2)}) collective-permute-start(bf16[128,8192]{1,0:T(8,128)(2,1)} %bitcast.65), channel_id=1, source_target_pairs={{0,2},{1,3},{2,0},{3,1},{4,6},{5,7},{6,4},{7,5},{8,10},{9,11},{10,... | collective-permute-start | bytes 6291464 | tf_op jit(solution)/shard_map/ppermute | solution.py:155
  17.8 3.1 %collective-permute-start.2 = (bf16[128,8192]{1,0:T(8,128)(2,1)}, bf16[128,8192]{1,0:T(8,128)(2,1)}, u32[]{:S(2)}, u32[]{:S(2)}) collective-permute-start(bf16[128,8192]{1,0:T(8,128)(2,1)} %bitcast.66), channel_id=1, source_target_pairs={{0,3},{1,0},{2,1},{3,2},{4,7},{5,4},{6,5},{7,6},{8,11},{9,8},{10,9... | collective-permute-start | bytes 6291464 | tf_op jit(solution)/shard_map/ppermute | solution.py:155
  21.4 5.8 %cholesky.96 = f32[64,64]{1,0:T(8,128)S(1)} custom-call(f32[64,64]{1,0:T(8,128)S(1)} %fusion.50), custom_call_target="Cholesky" | custom-call | tf_op jit(solution)/shard_map/jit(cholesky)/cholesky | solution.py:23
  27.9 0.7 fusion.43
  28.6 4.9 %custom-call.12 = f32[1,64,64]{1,2,0:T(8,128)S(1)} custom-call(f32[1,64,64]{2,1,0:T(8,128)S(1)} %fusion.43), custom_call_target="InvertDiagBlocksLowerTriangular" | custom-call | tf_op jit(solution)/shard_map/triangular_solve/custom-call.2 | solution.py:24
  34.4 5.9 %cholesky.107 = f32[64,64]{1,0:T(8,128)S(1)} custom-call(f32[64,64]{1,0:T(8,128)S(1)} %fusion.48), custom_call_target="Cholesky" | custom-call | tf_op jit(solution)/shard_map/jit(cholesky)/cholesky | solution.py:23
  41.6 4.9 %custom-call.13 = f32[1,64,64]{1,2,0:T(8,128)S(1)} custom-call(f32[1,64,64]{2,1,0:T(8,128)S(1)} %fusion.44), custom_call_target="InvertDiagBlocksLowerTriangular" | custom-call | tf_op jit(solution)/shard_map/triangular_solve/custom-call.2 | solution.py:24
  46.5 1.1 convolution_bitcast_fusion
  47.6 116.8 %all-gather.2.cloned.1.call-done = bf16[8192,448]{1,0:T(8,128)(2,1)} async-done(((bf16[64,448]{1,0:T(8,128)(2,1)}), bf16[8192,448]{1,0:T(8,128)(2,1)}) %all-gather.2.cloned.1.call-update) | async-done | bytes 7340048 | tf_op jit(solution)/shard_map/all_gather | solution.py:149
  164.3 5.0 %fusion.13 = f32[192,192]{0,1:T(8,128)S(1)} fusion(bf16[8192,448]{1,0:T(8,128)(2,1)} %all-gather.2.cloned.1.call-done), kind=kOutput, calls=%fused_computation.13 | convolution fusion | flops 603979776 | bytes 4341760 | tf_op jit(solution)/shard_map/dot_general | solution.py:103
  169.6 5.8 %cholesky.74 = f32[64,64]{1,0:T(8,128)S(1)} custom-call(f32[64,64]{1,0:T(8,128)S(1)} %fusion.54), custom_call_target="Cholesky" | custom-call | tf_op jit(solution)/shard_map/jit(cholesky)/cholesky | solution.py:93
  176.8 4.9 %custom-call.10 = f32[1,64,64]{1,2,0:T(8,128)S(1)} custom-call(f32[1,64,64]{2,1,0:T(8,128)S(1)} %fusion.41), custom_call_target="InvertDiagBlocksLowerTriangular" | custom-call | tf_op jit(solution)/shard_map/triangular_solve/custom-call.0 | solution.py:92
  182.5 5.8 %cholesky.85 = f32[64,64]{1,0:T(8,128)S(1)} custom-call(f32[64,64]{1,0:T(8,128)S(1)} %fusion.52), custom_call_target="Cholesky" | custom-call | tf_op jit(solution)/shard_map/jit(cholesky)/cholesky | solution.py:97
  189.7 4.9 %custom-call.11 = f32[1,64,64]{1,2,0:T(8,128)S(1)} custom-call(f32[1,64,64]{2,1,0:T(8,128)S(1)} %fusion.42), custom_call_target="InvertDiagBlocksLowerTriangular" | custom-call | tf_op jit(solution)/shard_map/triangular_solve/custom-call.0 | solution.py:96
  195.1 3.8 %fusion.11 = f32[8192,192]{0,1:T(8,128)S(1)} fusion(bf16[8192,448]{1,0:T(8,128)(2,1)} %all-gather.2.cloned.1.call-done, bf16[64,64]{1,0:T(8,128)(2,1)S(1)} %get-tuple-element.13, bf16[64,64]{1,0:T(8,128)(2,1)S(1)} %broadcast_in_dim.7, bf16[64,64]{1,0:T(8,128)(2,1)S(1)} %get-tuple-element.12, bf16[64,64]{1,0:T(8,128)(2,1)S(1)} %get-tuple-element.11), kind=kOutput, calls=%fused_computation.11 | convolution fusion | flops 604569600 | bytes 10518528 | tf_op jit(solution)/shard_map/dot_general | solution.py:123
  199.3 2.0 copy.50
  201.3 2.2 slice-done
  203.4 0.7 copy-done.1
  204.7 5.6 %fusion = f32[512,320]{0,1:T(8,128)S(1)} fusion(bf16[128,8192]{1,0:T(8,128)(2,1)} %collective-permute-done.2, bf16[128,8192]{1,0:T(8,128)(2,1)} %collective-permute-done.1, bf16[128,8192]{1,0:T(8,128)(2,1)} %collective-permute-done, bf16[128,8192]{1,0:T(8,128)(2,1)S(1)} %bitcast.67, bf16[8192,64]{1,0:T(8,128)(2,1)S(1)} %copy-done.1, ...), kind=kOutput, calls=%fused_computation | convolution fusion | flops 2728394752 | bytes 14286848 | tf_op jit(solution)/shard_map/dot_general | solution.py:167
  210.3 0.8 copy-done.3
  211.4 1.5 convolution_multiply_fusion
  213.2 0.8 constant_dynamic-slice_fusion.k_ref
  214.0 14.1 %shard_map.68 = f32[16,2,512]{2,1,0:T(2,128)} custom-call(bf16[512,2048]{1,0:T(8,128)(2,1)} %bitcast.63, bf16[2,512,256]{2,1,0:T(8,128)(2,1)} %constant_dynamic-slice_fusion.k_ref), custom_call_target="tpu_custom_call" | custom-call | tf_op jit(solution)/shard_map/pallas_call | solution.py:77
  228.2 1.0 reduce_sum.27
  229.2 0.7 broadcast_in_dim.8
  229.8 9.6 %all-to-all-start = ((f32[128,1,2]{2,1,0:T(1,128)}), f32[128,1,2]{2,1,0:T(1,128)S(1)}, u32[]{:S(2)}, u32[]{:S(2)}) async-start(f32[128,1,2]{2,1,0:T(1,128)} %broadcast_in_dim.8), calls=%async_computation | async-start | bytes 131072 | tf_op jit(solution)/shard_map/all_to_all | solution.py:138
  239.5 1.2 convolution_multiply_fusion.1
  240.7 13.7 %all-to-all-done = f32[128,1,2]{2,1,0:T(1,128)S(1)} async-done(((f32[128,1,2]{2,1,0:T(1,128)}), f32[128,1,2]{2,1,0:T(1,128)S(1)}, u32[]{:S(2)}, u32[]{:S(2)}) %all-to-all-start) | async-done | bytes 1056 | tf_op jit(solution)/shard_map/all_to_all | solution.py:138
  254.5 7.9 %all_to_all.12 = f32[4,1,2]{2,1,0:T(1,128)S(1)} all-to-all(f32[4,1,2]{2,1,0:T(1,128)S(1)} %broadcast_in_dim.9), channel_id=1, replica_groups=mesh['fsdp'=128,'seq'=4] {'seq'}, dimensions={0} | all-to-all | bytes 64 | tf_op jit(solution)/shard_map/all_to_all | solution.py:138
  (59 shorter events, 9.6 us)
Async XLA Ops:
  7.2 13.8 %copy-start = (f32[1024,64]{0,1:T(8,128)S(1)}, f32[1024,64]{0,1:T(8,128)}, u32[]{:S(2)}) copy-start(f32[1024,64]{0,1:T(8,128)} %param.14) | copy-start | bytes 786436
  7.2 157.2 %all-gather.2.cloned.1.call-start = ((), (), s32[]{:S(2)}) async-start(), calls=%async_computation.2 | async-start | bytes 8454144 | tf_op jit(solution)/shard_map/all_gather | solution.py:149
  9.5 191.7 %collective-permute-start = (bf16[128,8192]{1,0:T(8,128)(2,1)}, bf16[128,8192]{1,0:T(8,128)(2,1)}, u32[]{:S(2)}, u32[]{:S(2)}) collective-permute-start(bf16[128,8192]{1,0:T(8,128)(2,1)} %bitcast.64), channel_id=1, source_target_pairs={{0,1},{1,2},{2,3},{3,0},{4,5},{5,6},{6,7},{7,4},{8,9},{9,10},{10,1... | collective-permute-start | bytes 6291464 | tf_op jit(solution)/shard_map/ppermute | solution.py:155
  13.5 187.8 %collective-permute-start.1 = (bf16[128,8192]{1,0:T(8,128)(2,1)}, bf16[128,8192]{1,0:T(8,128)(2,1)}, u32[]{:S(2)}, u32[]{:S(2)}) collective-permute-start(bf16[128,8192]{1,0:T(8,128)(2,1)} %bitcast.65), channel_id=1, source_target_pairs={{0,2},{1,3},{2,0},{3,1},{4,6},{5,7},{6,4},{7,5},{8,10},{9,11},{10,... | collective-permute-start | bytes 6291464 | tf_op jit(solution)/shard_map/ppermute | solution.py:155
  17.8 183.4 %collective-permute-start.2 = (bf16[128,8192]{1,0:T(8,128)(2,1)}, bf16[128,8192]{1,0:T(8,128)(2,1)}, u32[]{:S(2)}, u32[]{:S(2)}) collective-permute-start(bf16[128,8192]{1,0:T(8,128)(2,1)} %bitcast.66), channel_id=1, source_target_pairs={{0,3},{1,0},{2,1},{3,2},{4,7},{5,4},{6,5},{7,6},{8,11},{9,8},{10,9... | collective-permute-start | bytes 6291464 | tf_op jit(solution)/shard_map/ppermute | solution.py:155
  201.2 2.2 slice-start
  201.3 2.9 %copy-start.1 = (bf16[8192,64]{1,0:T(8,128)(2,1)S(1)}, bf16[8192,64]{1,0:T(8,128)(2,1)}, u32[]{:S(2)}) copy-start(bf16[8192,64]{1,0:T(8,128)(2,1)} %copy.50) | copy-start | bytes 3145732
  201.3 3.5 %copy-start.4 = (bf16[1,128,8192]{2,1,0:T(8,128)(2,1)S(1)}, bf16[1,128,8192]{2,1,0:T(8,128)(2,1)}, u32[]{:S(2)}) copy-start(bf16[1,128,8192]{2,1,0:T(8,128)(2,1)} %param.10) | copy-start | bytes 6291460
  210.3 0.8 copy-start.3
  213.0 26.4 %copy-start.2 = (f32[1024,64]{0,1:T(8,128)S(1)}, f32[1024,64]{0,1:T(8,128)}, u32[]{:S(2)}) copy-start(f32[1024,64]{0,1:T(8,128)} %convolution_bitcast_fusion) | copy-start | bytes 786436
  229.8 24.5 %all-to-all-start = ((f32[128,1,2]{2,1,0:T(1,128)}), f32[128,1,2]{2,1,0:T(1,128)S(1)}, u32[]{:S(2)}, u32[]{:S(2)}) async-start(f32[128,1,2]{2,1,0:T(1,128)} %broadcast_in_dim.8), calls=%async_computation | async-start | bytes 131072 | tf_op jit(solution)/shard_map/all_to_all | solution.py:138
Sparse Core Ops, SparseCore 0:
  11.1 153.1 all-gather.1

commit v6 on v5

--- a/solution.py
+++ b/solution.py
@@ -102,7 +102,7 @@
 def gram_of_pieces(pieces, r):
     full = lax.dot_general(pieces, pieces, (((0,), (0,)), ((), ())), preferred_element_type=jnp.float32)
     block = lambda a, b: full[a * r : (a + 1) * r, b * r : (b + 1) * r]
-    order = [(2, 2), (2, 1), (1, 2), (1, 1), (0, 2), (2, 0), (0, 1), (1, 0), (0, 0)]
+    order = [(1, 1), (0, 1), (1, 0), (0, 0)]
     total = block(*order[0])
     for a, b in order[1:]:
         total = total + block(a, b)
@@ -116,7 +116,6 @@
         [
             jnp.concatenate([mh, mm, ml], axis=1),
             jnp.concatenate([mh, mm, zero], axis=1),
-            jnp.concatenate([mh, zero, zero], axis=1),
         ],
         axis=0,
     )
@@ -145,7 +144,7 @@
     slice_width = key_weight.shape[1]
     rows = u_factor.shape[0]
 
-    packed = jnp.concatenate([key_weight] + split3(u_factor), axis=1)
+    packed = jnp.concatenate([key_weight] + split3(u_factor)[:2], axis=1)
     whole = lax.all_gather(packed, "fsdp", axis=0, tiled=True)
 
     x_local = tokens[0]

time: 271 us -> 265 us (0.978)
  matrix products: 20.5 us -> 17.3 us
  waiting for transfers between devices: 130 us -> 127 us
    all_gather x1, waiting for transfers between devices: 117 us -> 114 us  [local(): whole = lax.all_gather(packed, 'fsdp', axis=0, tiled=True)]
  transfers between devices with their start and end apart: 5 -> 5, of which waited for: 2 -> 2; matrix products, arithmetic and copies ran while one was open for 24% -> 23% of each run, Pallas kernels for 0% -> 0%
where the time goes in v6:
time: 265 us; the launch traced here: 264 us
  waiting for transfers between devices  127 us (48%)
  other arithmetic  53 us (20%)
  starting transfers between devices  21.3 us (8%)
  matrix products  17.3 us (7%)
  between operations  14.4 us (5%)
  Pallas kernels  14.1 us (5%)
  local copies, waits for them, and re-layouts  8.31 us (3%)
  blocking collectives  7.91 us (3%)
    all_gather x1, waiting for transfers between devices, local(): whole = lax.all_gather(packed, 'fsdp', axis=0, tiled=True)  114 us
    pallas_call x1, Pallas kernels, lse_rows(): pl.pallas_call(kern, grid=(kv, GROUP), in_specs=[pl.BlockSpec((length, HD...  14.1 us
    all_to_all x1, waiting for transfers between devices, total_over(): return jnp.sum(lax.all_to_all(spread, axis, 0, 0, tiled=True), axis=0)  13.7 us
    another operation x6, other arithmetic, solve_rows(): lower = jnp.linalg.cholesky(gram)  13 us
    ppermute x3, starting transfers between devices, local(): lax.ppermute(x_local, 'seq', [(i, (i + shift) % n_seq) for i in range(n_s...  11.4 us
    another operation x4, other arithmetic, solve_rows(): lax.linalg.triangular_solve(lower, rows, left_side=False, lower=True, tra...  11.1 us
    all_to_all x1, starting transfers between devices, total_over(): return jnp.sum(lax.all_to_all(spread, axis, 0, 0, tiled=True), axis=0)  9.93 us
    all_to_all x1, blocking collectives, total_over(): return jnp.sum(lax.all_to_all(spread, axis, 0, 0, tiled=True), axis=0)  7.91 us
  transfers between devices with their start and end apart: 5, of which 2 were waited for; matrix products, arithmetic and copies ran while one was open for 23% of the time, Pallas kernels for 0%

profile of v6, /device:TPU:1, one launch (start us, length us, event | category | flops | bytes accessed | tf_op | source)
XLA Modules:
  0.0 263.8 jit_solution(1578095521123882479)
XLA Ops:
  7.2 0.8 reduce-precision_convert_fusion.2
  8.0 1.5 pad_maximum_fusion.1
  9.5 3.9 %collective-permute-start = (bf16[128,8192]{1,0:T(8,128)(2,1)}, bf16[128,8192]{1,0:T(8,128)(2,1)}, u32[]{:S(2)}, u32[]{:S(2)}) collective-permute-start(bf16[128,8192]{1,0:T(8,128)(2,1)} %bitcast.64), channel_id=1, source_target_pairs={{0,1},{1,2},{2,3},{3,0},{4,5},{5,6},{6,7},{7,4},{8,9},{9,10},{10,1... | collective-permute-start | bytes 6291464 | tf_op jit(solution)/shard_map/ppermute | solution.py:154
  13.4 4.4 %collective-permute-start.1 = (bf16[128,8192]{1,0:T(8,128)(2,1)}, bf16[128,8192]{1,0:T(8,128)(2,1)}, u32[]{:S(2)}, u32[]{:S(2)}) collective-permute-start(bf16[128,8192]{1,0:T(8,128)(2,1)} %bitcast.65), channel_id=1, source_target_pairs={{0,2},{1,3},{2,0},{3,1},{4,6},{5,7},{6,4},{7,5},{8,10},{9,11},{10,... | collective-permute-start | bytes 6291464 | tf_op jit(solution)/shard_map/ppermute | solution.py:154
  17.8 3.1 %collective-permute-start.2 = (bf16[128,8192]{1,0:T(8,128)(2,1)}, bf16[128,8192]{1,0:T(8,128)(2,1)}, u32[]{:S(2)}, u32[]{:S(2)}) collective-permute-start(bf16[128,8192]{1,0:T(8,128)(2,1)} %bitcast.66), channel_id=1, source_target_pairs={{0,3},{1,0},{2,1},{3,2},{4,7},{5,4},{6,5},{7,6},{8,11},{9,8},{10,9... | collective-permute-start | bytes 6291464 | tf_op jit(solution)/shard_map/ppermute | solution.py:154
  21.4 5.8 %cholesky.96 = f32[64,64]{1,0:T(8,128)S(1)} custom-call(f32[64,64]{1,0:T(8,128)S(1)} %fusion.45), custom_call_target="Cholesky" | custom-call | tf_op jit(solution)/shard_map/jit(cholesky)/cholesky | solution.py:23
  28.6 4.9 %custom-call.12 = f32[1,64,64]{1,2,0:T(8,128)S(1)} custom-call(f32[1,64,64]{2,1,0:T(8,128)S(1)} %fusion.37), custom_call_target="InvertDiagBlocksLowerTriangular" | custom-call | tf_op jit(solution)/shard_map/triangular_solve/custom-call.2 | solution.py:24
  34.4 5.9 %cholesky.107 = f32[64,64]{1,0:T(8,128)S(1)} custom-call(f32[64,64]{1,0:T(8,128)S(1)} %fusion.43), custom_call_target="Cholesky" | custom-call | tf_op jit(solution)/shard_map/jit(cholesky)/cholesky | solution.py:23
  40.9 0.7 fusion.38
  41.5 4.9 %custom-call.13 = f32[1,64,64]{1,2,0:T(8,128)S(1)} custom-call(f32[1,64,64]{2,1,0:T(8,128)S(1)} %fusion.38), custom_call_target="InvertDiagBlocksLowerTriangular" | custom-call | tf_op jit(solution)/shard_map/triangular_solve/custom-call.2 | solution.py:24
  46.4 1.1 convolution_bitcast_fusion
  47.6 113.7 %all-gather.2.cloned.1.call-done = bf16[8192,384]{1,0:T(8,128)(2,1)} async-done(((bf16[64,384]{1,0:T(8,128)(2,1)}), bf16[8192,384]{1,0:T(8,128)(2,1)}) %all-gather.2.cloned.1.call-update) | async-done | bytes 6291472 | tf_op jit(solution)/shard_map/all_gather | solution.py:148
  161.2 3.0 %fusion.13 = f32[128,128]{0,1:T(8,128)S(1)} fusion(bf16[8192,384]{1,0:T(8,128)(2,1)} %all-gather.2.cloned.1.call-done), kind=kOutput, calls=%fused_computation.15 | convolution fusion | flops 268435456 | bytes 2162688 | tf_op jit(solution)/shard_map/dot_general | solution.py:103
  164.5 5.8 %cholesky.74 = f32[64,64]{1,0:T(8,128)S(1)} custom-call(f32[64,64]{1,0:T(8,128)S(1)} %fusion.49), custom_call_target="Cholesky" | custom-call | tf_op jit(solution)/shard_map/jit(cholesky)/cholesky | solution.py:93
  171.7 4.9 %custom-call.10 = f32[1,64,64]{1,2,0:T(8,128)S(1)} custom-call(f32[1,64,64]{2,1,0:T(8,128)S(1)} %fusion.35), custom_call_target="InvertDiagBlocksLowerTriangular" | custom-call | tf_op jit(solution)/shard_map/triangular_solve/custom-call.0 | solution.py:92
  177.3 5.8 %cholesky.85 = f32[64,64]{1,0:T(8,128)S(1)} custom-call(f32[64,64]{1,0:T(8,128)S(1)} %fusion.47), custom_call_target="Cholesky" | custom-call | tf_op jit(solution)/shard_map/jit(cholesky)/cholesky | solution.py:97
  184.5 4.9 %custom-call.11 = f32[1,64,64]{1,2,0:T(8,128)S(1)} custom-call(f32[1,64,64]{2,1,0:T(8,128)S(1)} %fusion.36), custom_call_target="InvertDiagBlocksLowerTriangular" | custom-call | tf_op jit(solution)/shard_map/triangular_solve/custom-call.0 | solution.py:96
  189.9 2.7 %fusion.11 = f32[8192,192]{0,1:T(8,128)S(1)} fusion(bf16[8192,384]{1,0:T(8,128)(2,1)} %all-gather.2.cloned.1.call-done, bf16[64,64]{1,0:T(8,128)(2,1)S(1)} %broadcast_in_dim.7, bf16[64,64]{1,0:T(8,128)(2,1)S(1)} %get-tuple-element.12, bf16[64,64]{1,0:T(8,128)(2,1)S(1)} %get-tuple-element.13, bf16[64,64]{1,0:T(8,128)(2,1)S(1)} %get-tuple-element.11), kind=kOutput, calls=%fused_computation.13 | convolution fusion | flops 402948096 | bytes 8421376 | tf_op jit(solution)/shard_map/dot_general | solution.py:122
  193.0 2.0 copy.35
  195.0 2.2 slice-done
  197.1 0.7 copy-done.1
  198.4 5.6 %fusion = f32[512,320]{0,1:T(8,128)S(1)} fusion(bf16[128,8192]{1,0:T(8,128)(2,1)} %collective-permute-done.2, bf16[128,8192]{1,0:T(8,128)(2,1)} %collective-permute-done.1, bf16[128,8192]{1,0:T(8,128)(2,1)} %collective-permute-done, bf16[128,8192]{1,0:T(8,128)(2,1)S(1)} %bitcast.67, bf16[8192,64]{1,0:T(8,128)(2,1)S(1)} %copy-done.1, ...), kind=kOutput, calls=%fused_computation | convolution fusion | flops 2728394752 | bytes 14286848 | tf_op jit(solution)/shard_map/dot_general | solution.py:166
  204.0 0.8 copy-done.3
  205.1 1.5 convolution_multiply_fusion
  206.9 0.8 constant_dynamic-slice_fusion.k_ref
  207.7 14.1 %shard_map.68 = f32[16,2,512]{2,1,0:T(2,128)} custom-call(bf16[512,2048]{1,0:T(8,128)(2,1)} %bitcast.63, bf16[2,512,256]{2,1,0:T(8,128)(2,1)} %constant_dynamic-slice_fusion.k_ref), custom_call_target="tpu_custom_call" | custom-call | tf_op jit(solution)/shard_map/pallas_call | solution.py:77
  221.8 1.0 reduce_sum.27
  222.9 0.7 broadcast_in_dim.8
  223.5 9.9 %all-to-all-start = ((f32[128,1,2]{2,1,0:T(1,128)}), f32[128,1,2]{2,1,0:T(1,128)S(1)}, u32[]{:S(2)}, u32[]{:S(2)}) async-start(f32[128,1,2]{2,1,0:T(1,128)} %broadcast_in_dim.8), calls=%async_computation | async-start | bytes 131072 | tf_op jit(solution)/shard_map/all_to_all | solution.py:137
  233.5 1.2 convolution_multiply_fusion.1
  234.7 13.7 %all-to-all-done = f32[128,1,2]{2,1,0:T(1,128)S(1)} async-done(((f32[128,1,2]{2,1,0:T(1,128)}), f32[128,1,2]{2,1,0:T(1,128)S(1)}, u32[]{:S(2)}, u32[]{:S(2)}) %all-to-all-start) | async-done | bytes 1056 | tf_op jit(solution)/shard_map/all_to_all | solution.py:137
  248.5 7.9 %all_to_all.12 = f32[4,1,2]{2,1,0:T(1,128)S(1)} all-to-all(f32[4,1,2]{2,1,0:T(1,128)S(1)} %broadcast_in_dim.9), channel_id=1, replica_groups=mesh['fsdp'=128,'seq'=4] {'seq'}, dimensions={0} | all-to-all | bytes 64 | tf_op jit(solution)/shard_map/all_to_all | solution.py:137
  (59 shorter events, 9.6 us)
Async XLA Ops:
  7.2 13.7 %copy-start = (f32[1024,64]{0,1:T(8,128)S(1)}, f32[1024,64]{0,1:T(8,128)}, u32[]{:S(2)}) copy-start(f32[1024,64]{0,1:T(8,128)} %param.14) | copy-start | bytes 786436
  7.2 154.1 %all-gather.2.cloned.1.call-start = ((), (), s32[]{:S(2)}) async-start(), calls=%async_computation.2 | async-start | bytes 6340608 | tf_op jit(solution)/shard_map/all_gather | solution.py:148
  9.5 185.4 %collective-permute-start = (bf16[128,8192]{1,0:T(8,128)(2,1)}, bf16[128,8192]{1,0:T(8,128)(2,1)}, u32[]{:S(2)}, u32[]{:S(2)}) collective-permute-start(bf16[128,8192]{1,0:T(8,128)(2,1)} %bitcast.64), channel_id=1, source_target_pairs={{0,1},{1,2},{2,3},{3,0},{4,5},{5,6},{6,7},{7,4},{8,9},{9,10},{10,1... | collective-permute-start | bytes 6291464 | tf_op jit(solution)/shard_map/ppermute | solution.py:154
  13.4 181.5 %collective-permute-start.1 = (bf16[128,8192]{1,0:T(8,128)(2,1)}, bf16[128,8192]{1,0:T(8,128)(2,1)}, u32[]{:S(2)}, u32[]{:S(2)}) collective-permute-start(bf16[128,8192]{1,0:T(8,128)(2,1)} %bitcast.65), channel_id=1, source_target_pairs={{0,2},{1,3},{2,0},{3,1},{4,6},{5,7},{6,4},{7,5},{8,10},{9,11},{10,... | collective-permute-start | bytes 6291464 | tf_op jit(solution)/shard_map/ppermute | solution.py:154
  17.8 177.1 %collective-permute-start.2 = (bf16[128,8192]{1,0:T(8,128)(2,1)}, bf16[128,8192]{1,0:T(8,128)(2,1)}, u32[]{:S(2)}, u32[]{:S(2)}) collective-permute-start(bf16[128,8192]{1,0:T(8,128)(2,1)} %bitcast.66), channel_id=1, source_target_pairs={{0,3},{1,0},{2,1},{3,2},{4,7},{5,4},{6,5},{7,6},{8,11},{9,8},{10,9... | collective-permute-start | bytes 6291464 | tf_op jit(solution)/shard_map/ppermute | solution.py:154
  194.9 2.2 slice-start
  194.9 2.9 %copy-start.1 = (bf16[8192,64]{1,0:T(8,128)(2,1)S(1)}, bf16[8192,64]{1,0:T(8,128)(2,1)}, u32[]{:S(2)}) copy-start(bf16[8192,64]{1,0:T(8,128)(2,1)} %copy.35) | copy-start | bytes 3145732
  194.9 3.5 %copy-start.4 = (bf16[1,128,8192]{2,1,0:T(8,128)(2,1)S(1)}, bf16[1,128,8192]{2,1,0:T(8,128)(2,1)}, u32[]{:S(2)}) copy-start(bf16[1,128,8192]{2,1,0:T(8,128)(2,1)} %param.10) | copy-start | bytes 6291460
  204.0 0.8 copy-start.3
  206.7 26.7 %copy-start.2 = (f32[1024,64]{0,1:T(8,128)S(1)}, f32[1024,64]{0,1:T(8,128)}, u32[]{:S(2)}) copy-start(f32[1024,64]{0,1:T(8,128)} %convolution_bitcast_fusion) | copy-start | bytes 786436
  223.5 24.8 %all-to-all-start = ((f32[128,1,2]{2,1,0:T(1,128)}), f32[128,1,2]{2,1,0:T(1,128)S(1)}, u32[]{:S(2)}, u32[]{:S(2)}) async-start(f32[128,1,2]{2,1,0:T(1,128)} %broadcast_in_dim.8), calls=%async_computation | async-start | bytes 131072 | tf_op jit(solution)/shard_map/all_to_all | solution.py:137
Sparse Core Ops, SparseCore 0:
  11.1 150.0 all-gather.1

commit v7 on v6

--- a/solution.py
+++ b/solution.py
@@ -44,28 +44,33 @@
 
 
 def lse_kernel(q_ref, k_ref, o_ref, *, blk, n_blk, scale):
-    for p in range(2):
-        for qb in range(n_blk):
-            q_blk = q_ref[qb * blk:(qb + 1) * blk, :]
-            m = None
-            l = None
-            for kb in range(qb + 1):
-                k_blk = k_ref[p, kb * blk:(kb + 1) * blk, :]
-                s = lax.dot_general(k_blk, q_blk, (((1,), (1,)), ((), ())),
-                                    preferred_element_type=jnp.float32) * scale
-                if kb == qb:
-                    rows = lax.broadcasted_iota(jnp.int32, s.shape, 0)
-                    cols = lax.broadcasted_iota(jnp.int32, s.shape, 1)
-                    s = jnp.where(rows <= cols, s, -1e30)
-                top = jnp.max(s, axis=0, keepdims=True)
-                if m is None:
-                    m = top
-                    l = jnp.sum(jnp.exp(s - m), axis=0, keepdims=True)
-                else:
-                    m_new = jnp.maximum(m, top)
-                    l = l * jnp.exp(m - m_new) + jnp.sum(jnp.exp(s - m_new), axis=0, keepdims=True)
-                    m = m_new
-            o_ref[0, p:p + 1, qb * blk:(qb + 1) * blk] = m + jnp.log(l)
+    def one_head(g, carry):
+        col = pl.multiple_of(g * HD, HD)
+        for p in range(2):
+            for qb in range(n_blk):
+                q_blk = q_ref[qb * blk:(qb + 1) * blk, pl.ds(col, HD)]
+                m = None
+                l = None
+                for kb in range(qb + 1):
+                    k_blk = k_ref[p, kb * blk:(kb + 1) * blk, :]
+                    s = lax.dot_general(k_blk, q_blk, (((1,), (1,)), ((), ())),
+                                        preferred_element_type=jnp.float32) * scale
+                    if kb == qb:
+                        rows = lax.broadcasted_iota(jnp.int32, s.shape, 0)
+                        cols = lax.broadcasted_iota(jnp.int32, s.shape, 1)
+                        s = jnp.where(rows <= cols, s, -1e30)
+                    top = jnp.max(s, axis=0, keepdims=True)
+                    if m is None:
+                        m = top
+                        l = jnp.sum(jnp.exp(s - m), axis=0, keepdims=True)
+                    else:
+                        m_new = jnp.maximum(m, top)
+                        l = l * jnp.exp(m - m_new) + jnp.sum(jnp.exp(s - m_new), axis=0, keepdims=True)
+                        m = m_new
+                o_ref[pl.ds(g, 1), p, qb * blk:(qb + 1) * blk] = (m + jnp.log(l))
+        return carry
+
+    lax.fori_loop(0, GROUP, one_head, 0)
 
 
 def lse_rows(query_rows, keys_nat, interpret=False):
@@ -76,12 +81,12 @@
     kern = functools.partial(lse_kernel, blk=blk, n_blk=length // blk, scale=1.0 / math.sqrt(HD))
     return pl.pallas_call(
         kern,
-        grid=(kv, GROUP),
+        grid=(kv,),
         in_specs=[
-            pl.BlockSpec((length, HD), lambda k, g: (0, k * GROUP + g)),
-            pl.BlockSpec((2, length, HD), lambda k, g: (0, 0, k)),
+            pl.BlockSpec((length, GROUP * HD), lambda k: (0, k)),
+            pl.BlockSpec((2, length, HD), lambda k: (0, 0, k)),
         ],
-        out_specs=pl.BlockSpec((1, 2, length), lambda k, g: (k * GROUP + g, 0, 0)),
+        out_specs=pl.BlockSpec((GROUP, 2, length), lambda k: (k, 0, 0)),
         out_shape=jax.ShapeDtypeStruct((heads, 2, length), jnp.float32),
         interpret=interpret,
     )(query_rows, keys_nat)

time: 265 us -> 263 us (level)
  no operation moved by 1% of the time
where the time goes in v7:
time: 263 us; the launch traced here: 262 us
  waiting for transfers between devices  127 us (48%)
  other arithmetic  53 us (20%)
  starting transfers between devices  21.3 us (8%)
  matrix products  17.3 us (7%)
  between operations  14.4 us (5%)
  Pallas kernels  12.6 us (5%)
  local copies, waits for them, and re-layouts  8.31 us (3%)
  blocking collectives  7.91 us (3%)
    all_gather x1, waiting for transfers between devices, local(): whole = lax.all_gather(packed, 'fsdp', axis=0, tiled=True)  114 us
    all_to_all x1, waiting for transfers between devices, total_over(): return jnp.sum(lax.all_to_all(spread, axis, 0, 0, tiled=True), axis=0)  13.7 us
    another operation x6, other arithmetic, solve_rows(): lower = jnp.linalg.cholesky(gram)  13 us
    pallas_call x1, Pallas kernels, lse_rows(): pl.pallas_call(kern, grid=(kv,), in_specs=[pl.BlockSpec((length, GROUP *...  12.6 us
    ppermute x3, starting transfers between devices, local(): lax.ppermute(x_local, 'seq', [(i, (i + shift) % n_seq) for i in range(n_s...  11.4 us
    another operation x4, other arithmetic, solve_rows(): lax.linalg.triangular_solve(lower, rows, left_side=False, lower=True, tra...  11.1 us
    all_to_all x1, starting transfers between devices, total_over(): return jnp.sum(lax.all_to_all(spread, axis, 0, 0, tiled=True), axis=0)  9.93 us
    all_to_all x1, blocking collectives, total_over(): return jnp.sum(lax.all_to_all(spread, axis, 0, 0, tiled=True), axis=0)  7.91 us
  transfers between devices with their start and end apart: 5, of which 2 were waited for; matrix products, arithmetic and copies ran while one was open for 23% of the time, Pallas kernels for 0%

profile of v7, /device:TPU:1, one launch (start us, length us, event | category | flops | bytes accessed | tf_op | source)
XLA Modules:
  0.0 262.2 jit_solution(34032409009030744)
XLA Ops:
  7.2 0.8 reduce-precision_convert_fusion.2
  8.0 1.5 pad_maximum_fusion.1
  9.5 3.9 %collective-permute-start = (bf16[128,8192]{1,0:T(8,128)(2,1)}, bf16[128,8192]{1,0:T(8,128)(2,1)}, u32[]{:S(2)}, u32[]{:S(2)}) collective-permute-start(bf16[128,8192]{1,0:T(8,128)(2,1)} %bitcast.64), channel_id=1, source_target_pairs={{0,1},{1,2},{2,3},{3,0},{4,5},{5,6},{6,7},{7,4},{8,9},{9,10},{10,1... | collective-permute-start | bytes 6291464 | tf_op jit(solution)/shard_map/ppermute | solution.py:159
  13.4 4.4 %collective-permute-start.1 = (bf16[128,8192]{1,0:T(8,128)(2,1)}, bf16[128,8192]{1,0:T(8,128)(2,1)}, u32[]{:S(2)}, u32[]{:S(2)}) collective-permute-start(bf16[128,8192]{1,0:T(8,128)(2,1)} %bitcast.65), channel_id=1, source_target_pairs={{0,2},{1,3},{2,0},{3,1},{4,6},{5,7},{6,4},{7,5},{8,10},{9,11},{10,... | collective-permute-start | bytes 6291464 | tf_op jit(solution)/shard_map/ppermute | solution.py:159
  17.8 3.1 %collective-permute-start.2 = (bf16[128,8192]{1,0:T(8,128)(2,1)}, bf16[128,8192]{1,0:T(8,128)(2,1)}, u32[]{:S(2)}, u32[]{:S(2)}) collective-permute-start(bf16[128,8192]{1,0:T(8,128)(2,1)} %bitcast.66), channel_id=1, source_target_pairs={{0,3},{1,0},{2,1},{3,2},{4,7},{5,4},{6,5},{7,6},{8,11},{9,8},{10,9... | collective-permute-start | bytes 6291464 | tf_op jit(solution)/shard_map/ppermute | solution.py:159
  21.4 5.8 %cholesky.96 = f32[64,64]{1,0:T(8,128)S(1)} custom-call(f32[64,64]{1,0:T(8,128)S(1)} %fusion.45), custom_call_target="Cholesky" | custom-call | tf_op jit(solution)/shard_map/jit(cholesky)/cholesky | solution.py:23
  28.6 4.9 %custom-call.12 = f32[1,64,64]{1,2,0:T(8,128)S(1)} custom-call(f32[1,64,64]{2,1,0:T(8,128)S(1)} %fusion.37), custom_call_target="InvertDiagBlocksLowerTriangular" | custom-call | tf_op jit(solution)/shard_map/triangular_solve/custom-call.2 | solution.py:24
  34.4 5.9 %cholesky.107 = f32[64,64]{1,0:T(8,128)S(1)} custom-call(f32[64,64]{1,0:T(8,128)S(1)} %fusion.43), custom_call_target="Cholesky" | custom-call | tf_op jit(solution)/shard_map/jit(cholesky)/cholesky | solution.py:23
  40.9 0.7 fusion.38
  41.5 4.9 %custom-call.13 = f32[1,64,64]{1,2,0:T(8,128)S(1)} custom-call(f32[1,64,64]{2,1,0:T(8,128)S(1)} %fusion.38), custom_call_target="InvertDiagBlocksLowerTriangular" | custom-call | tf_op jit(solution)/shard_map/triangular_solve/custom-call.2 | solution.py:24
  46.4 1.1 convolution_bitcast_fusion
  47.6 113.7 %all-gather.2.cloned.1.call-done = bf16[8192,384]{1,0:T(8,128)(2,1)} async-done(((bf16[64,384]{1,0:T(8,128)(2,1)}), bf16[8192,384]{1,0:T(8,128)(2,1)}) %all-gather.2.cloned.1.call-update) | async-done | bytes 6291472 | tf_op jit(solution)/shard_map/all_gather | solution.py:153
  161.2 3.0 %fusion.13 = f32[128,128]{0,1:T(8,128)S(1)} fusion(bf16[8192,384]{1,0:T(8,128)(2,1)} %all-gather.2.cloned.1.call-done), kind=kOutput, calls=%fused_computation.15 | convolution fusion | flops 268435456 | bytes 2162688 | tf_op jit(solution)/shard_map/dot_general | solution.py:108
  164.5 5.8 %cholesky.74 = f32[64,64]{1,0:T(8,128)S(1)} custom-call(f32[64,64]{1,0:T(8,128)S(1)} %fusion.49), custom_call_target="Cholesky" | custom-call | tf_op jit(solution)/shard_map/jit(cholesky)/cholesky | solution.py:98
  171.7 4.9 %custom-call.10 = f32[1,64,64]{1,2,0:T(8,128)S(1)} custom-call(f32[1,64,64]{2,1,0:T(8,128)S(1)} %fusion.35), custom_call_target="InvertDiagBlocksLowerTriangular" | custom-call | tf_op jit(solution)/shard_map/triangular_solve/custom-call.0 | solution.py:97
  177.3 5.8 %cholesky.85 = f32[64,64]{1,0:T(8,128)S(1)} custom-call(f32[64,64]{1,0:T(8,128)S(1)} %fusion.47), custom_call_target="Cholesky" | custom-call | tf_op jit(solution)/shard_map/jit(cholesky)/cholesky | solution.py:102
  184.5 4.9 %custom-call.11 = f32[1,64,64]{1,2,0:T(8,128)S(1)} custom-call(f32[1,64,64]{2,1,0:T(8,128)S(1)} %fusion.36), custom_call_target="InvertDiagBlocksLowerTriangular" | custom-call | tf_op jit(solution)/shard_map/triangular_solve/custom-call.0 | solution.py:101
  189.9 2.7 %fusion.11 = f32[8192,192]{0,1:T(8,128)S(1)} fusion(bf16[8192,384]{1,0:T(8,128)(2,1)} %all-gather.2.cloned.1.call-done, bf16[64,64]{1,0:T(8,128)(2,1)S(1)} %broadcast_in_dim.7, bf16[64,64]{1,0:T(8,128)(2,1)S(1)} %get-tuple-element.12, bf16[64,64]{1,0:T(8,128)(2,1)S(1)} %get-tuple-element.13, bf16[64,64]{1,0:T(8,128)(2,1)S(1)} %get-tuple-element.11), kind=kOutput, calls=%fused_computation.13 | convolution fusion | flops 402948096 | bytes 8421376 | tf_op jit(solution)/shard_map/dot_general | solution.py:127
  193.0 2.0 copy.35
  195.0 2.2 slice-done
  197.1 0.7 copy-done.1
  198.4 5.6 %fusion = f32[512,320]{0,1:T(8,128)S(1)} fusion(bf16[128,8192]{1,0:T(8,128)(2,1)} %collective-permute-done.2, bf16[128,8192]{1,0:T(8,128)(2,1)} %collective-permute-done.1, bf16[128,8192]{1,0:T(8,128)(2,1)} %collective-permute-done, bf16[128,8192]{1,0:T(8,128)(2,1)S(1)} %bitcast.67, bf16[8192,64]{1,0:T(8,128)(2,1)S(1)} %copy-done.1, ...), kind=kOutput, calls=%fused_computation | convolution fusion | flops 2728394752 | bytes 14286848 | tf_op jit(solution)/shard_map/dot_general | solution.py:171
  204.0 0.8 copy-done.3
  205.1 1.5 convolution_multiply_fusion
  206.9 0.8 constant_dynamic-slice_fusion.k_ref
  207.7 12.6 %shard_map.68 = f32[16,2,512]{2,1,0:T(2,128)} custom-call(bf16[512,2048]{1,0:T(8,128)(2,1)} %bitcast.63, bf16[2,512,256]{2,1,0:T(8,128)(2,1)} %constant_dynamic-slice_fusion.k_ref), custom_call_target="tpu_custom_call" | custom-call | tf_op jit(solution)/shard_map/pallas_call | solution.py:82
  220.3 1.0 reduce_sum.27
  221.3 0.7 broadcast_in_dim.8
  222.0 9.9 %all-to-all-start = ((f32[128,1,2]{2,1,0:T(1,128)}), f32[128,1,2]{2,1,0:T(1,128)S(1)}, u32[]{:S(2)}, u32[]{:S(2)}) async-start(f32[128,1,2]{2,1,0:T(1,128)} %broadcast_in_dim.8), calls=%async_computation | async-start | bytes 131072 | tf_op jit(solution)/shard_map/all_to_all | solution.py:142
  231.9 1.2 convolution_multiply_fusion.1
  233.1 13.7 %all-to-all-done = f32[128,1,2]{2,1,0:T(1,128)S(1)} async-done(((f32[128,1,2]{2,1,0:T(1,128)}), f32[128,1,2]{2,1,0:T(1,128)S(1)}, u32[]{:S(2)}, u32[]{:S(2)}) %all-to-all-start) | async-done | bytes 1056 | tf_op jit(solution)/shard_map/all_to_all | solution.py:142
  246.9 7.9 %all_to_all.12 = f32[4,1,2]{2,1,0:T(1,128)S(1)} all-to-all(f32[4,1,2]{2,1,0:T(1,128)S(1)} %broadcast_in_dim.9), channel_id=1, replica_groups=mesh['fsdp'=128,'seq'=4] {'seq'}, dimensions={0} | all-to-all | bytes 64 | tf_op jit(solution)/shard_map/all_to_all | solution.py:142
  (59 shorter events, 9.6 us)
Async XLA Ops:
  7.2 13.7 %copy-start = (f32[1024,64]{0,1:T(8,128)S(1)}, f32[1024,64]{0,1:T(8,128)}, u32[]{:S(2)}) copy-start(f32[1024,64]{0,1:T(8,128)} %param.14) | copy-start | bytes 786436
  7.2 154.1 %all-gather.2.cloned.1.call-start = ((), (), s32[]{:S(2)}) async-start(), calls=%async_computation.2 | async-start | bytes 6340608 | tf_op jit(solution)/shard_map/all_gather | solution.py:153
  9.5 185.4 %collective-permute-start = (bf16[128,8192]{1,0:T(8,128)(2,1)}, bf16[128,8192]{1,0:T(8,128)(2,1)}, u32[]{:S(2)}, u32[]{:S(2)}) collective-permute-start(bf16[128,8192]{1,0:T(8,128)(2,1)} %bitcast.64), channel_id=1, source_target_pairs={{0,1},{1,2},{2,3},{3,0},{4,5},{5,6},{6,7},{7,4},{8,9},{9,10},{10,1... | collective-permute-start | bytes 6291464 | tf_op jit(solution)/shard_map/ppermute | solution.py:159
  13.4 181.5 %collective-permute-start.1 = (bf16[128,8192]{1,0:T(8,128)(2,1)}, bf16[128,8192]{1,0:T(8,128)(2,1)}, u32[]{:S(2)}, u32[]{:S(2)}) collective-permute-start(bf16[128,8192]{1,0:T(8,128)(2,1)} %bitcast.65), channel_id=1, source_target_pairs={{0,2},{1,3},{2,0},{3,1},{4,6},{5,7},{6,4},{7,5},{8,10},{9,11},{10,... | collective-permute-start | bytes 6291464 | tf_op jit(solution)/shard_map/ppermute | solution.py:159
  17.8 177.1 %collective-permute-start.2 = (bf16[128,8192]{1,0:T(8,128)(2,1)}, bf16[128,8192]{1,0:T(8,128)(2,1)}, u32[]{:S(2)}, u32[]{:S(2)}) collective-permute-start(bf16[128,8192]{1,0:T(8,128)(2,1)} %bitcast.66), channel_id=1, source_target_pairs={{0,3},{1,0},{2,1},{3,2},{4,7},{5,4},{6,5},{7,6},{8,11},{9,8},{10,9... | collective-permute-start | bytes 6291464 | tf_op jit(solution)/shard_map/ppermute | solution.py:159
  194.9 2.2 slice-start
  194.9 2.9 %copy-start.1 = (bf16[8192,64]{1,0:T(8,128)(2,1)S(1)}, bf16[8192,64]{1,0:T(8,128)(2,1)}, u32[]{:S(2)}) copy-start(bf16[8192,64]{1,0:T(8,128)(2,1)} %copy.35) | copy-start | bytes 3145732
  194.9 3.5 %copy-start.4 = (bf16[1,128,8192]{2,1,0:T(8,128)(2,1)S(1)}, bf16[1,128,8192]{2,1,0:T(8,128)(2,1)}, u32[]{:S(2)}) copy-start(bf16[1,128,8192]{2,1,0:T(8,128)(2,1)} %param.10) | copy-start | bytes 6291460
  204.0 0.8 copy-start.3
  206.7 25.2 %copy-start.2 = (f32[1024,64]{0,1:T(8,128)S(1)}, f32[1024,64]{0,1:T(8,128)}, u32[]{:S(2)}) copy-start(f32[1024,64]{0,1:T(8,128)} %convolution_bitcast_fusion) | copy-start | bytes 786436
  222.0 24.8 %all-to-all-start = ((f32[128,1,2]{2,1,0:T(1,128)}), f32[128,1,2]{2,1,0:T(1,128)S(1)}, u32[]{:S(2)}, u32[]{:S(2)}) async-start(f32[128,1,2]{2,1,0:T(1,128)} %broadcast_in_dim.8), calls=%async_computation | async-start | bytes 131072 | tf_op jit(solution)/shard_map/all_to_all | solution.py:142
Sparse Core Ops, SparseCore 0:
  11.1 150.0 all-gather.1

commit v8 on v7

--- a/solution.py
+++ b/solution.py
@@ -159,18 +159,17 @@
         chunks.append(lax.ppermute(x_local, "seq", [(i, (i + shift) % n_seq) for i in range(n_seq)]))
 
     q_v = orthonormal(v_factor)
-    weight_piece = whole[:, :slice_width]
     r = u_factor.shape[1]
     pieces = whole[:, slice_width:]
     q_u = apply_to_pieces(pieces, map_from_gram(gram_of_pieces(pieces, r)), r)
     q_low = q_u.astype(jnp.bfloat16)
-    both = jnp.concatenate([weight_piece, q_low], axis=1)
+    both = lax.dynamic_update_slice_in_dim(whole, q_low, slice_width, 1)
 
     col_start = me_seq * slice_width
     v_slice = lax.dynamic_slice_in_dim(q_v, col_start, slice_width, 0)
     prod = jnp.dot(jnp.concatenate(chunks, axis=0), both, preferred_element_type=jnp.float32)
     base = prod[:, :slice_width]
-    side = prod[:, slice_width:]
+    side = prod[:, slice_width : slice_width + r]
     offset = 2.0 * highest(side, v_slice.T)
     keys = jnp.stack([base + offset, base - offset]).astype(jnp.bfloat16)
     length = keys.shape[1]

time: 263 us -> 279 us (1.061)
  local copies, waits for them, and re-layouts: 8.31 us -> 21.9 us
    dynamic_update_slice x0 -> x1, local copies, waits for them, and re-layouts: none -> 18.1 us  [local(): both = lax.dynamic_update_slice_in_dim(whole, q_low, slice_width, 1)]
  transfers between devices with their start and end apart: 5 -> 5, of which waited for: 2 -> 2; matrix products, arithmetic and copies ran while one was open for 23% -> 29% of each run, Pallas kernels for 0% -> 0%
where the time goes in v8:
time: 279 us; the launch traced here: 278 us
  waiting for transfers between devices  128 us (46%)
  other arithmetic  54.3 us (19%)
  local copies, waits for them, and re-layouts  21.9 us (8%)
  starting transfers between devices  20.3 us (7%)
  matrix products  18.8 us (7%)
  between operations  14.4 us (5%)
  Pallas kernels  12.6 us (5%)
  blocking collectives  7.72 us (3%)
    all_gather x1, waiting for transfers between devices, local(): whole = lax.all_gather(packed, 'fsdp', axis=0, tiled=True)  115 us
    dynamic_update_slice x1, local copies, waits for them, and re-layouts, local(): both = lax.dynamic_update_slice_in_dim(whole, q_low, slice_width, 1)  18.1 us
    another operation x6, other arithmetic, solve_rows(): lower = jnp.linalg.cholesky(gram)  13 us
    all_to_all x1, waiting for transfers between devices, total_over(): return jnp.sum(lax.all_to_all(spread, axis, 0, 0, tiled=True), axis=0)  12.9 us
    pallas_call x1, Pallas kernels, lse_rows(): pl.pallas_call(kern, grid=(kv,), in_specs=[pl.BlockSpec((length, GROUP *...  12.6 us
    another operation x4, other arithmetic, solve_rows(): lax.linalg.triangular_solve(lower, rows, left_side=False, lower=True, tra...  11.1 us
    ppermute x3, starting transfers between devices, local(): lax.ppermute(x_local, 'seq', [(i, (i + shift) % n_seq) for i in range(n_s...  10.2 us
    all_to_all x1, starting transfers between devices, total_over(): return jnp.sum(lax.all_to_all(spread, axis, 0, 0, tiled=True), axis=0)  10.1 us
  transfers between devices with their start and end apart: 5, of which 2 were waited for; matrix products, arithmetic and copies ran while one was open for 29% of the time, Pallas kernels for 0%

profile of v8, /device:TPU:1, one launch (start us, length us, event | category | flops | bytes accessed | tf_op | source)
XLA Modules:
  0.0 278.1 jit_solution(3618093651216357423)
XLA Ops:
  7.2 0.8 reduce-precision_convert_fusion.2
  8.0 1.5 pad_maximum_fusion.1
  9.5 5.2 %collective-permute-start.2 = (bf16[128,8192]{1,0:T(8,128)(2,1)}, bf16[128,8192]{1,0:T(8,128)(2,1)}, u32[]{:S(2)}, u32[]{:S(2)}) collective-permute-start(bf16[128,8192]{1,0:T(8,128)(2,1)} %bitcast.65), channel_id=1, source_target_pairs={{0,3},{1,0},{2,1},{3,2},{4,7},{5,4},{6,5},{7,6},{8,11},{9,8},{10,9... | collective-permute-start | bytes 6291464 | tf_op jit(solution)/shard_map/ppermute | solution.py:159
  14.7 2.4 collective-permute-start.1
  17.2 2.5 collective-permute-start
  20.2 5.8 %cholesky.96 = f32[64,64]{1,0:T(8,128)S(1)} custom-call(f32[64,64]{1,0:T(8,128)S(1)} %fusion.42), custom_call_target="Cholesky" | custom-call | tf_op jit(solution)/shard_map/jit(cholesky)/cholesky | solution.py:23
  27.4 4.9 %custom-call.12 = f32[1,64,64]{1,2,0:T(8,128)S(1)} custom-call(f32[1,64,64]{2,1,0:T(8,128)S(1)} %fusion.34), custom_call_target="InvertDiagBlocksLowerTriangular" | custom-call | tf_op jit(solution)/shard_map/triangular_solve/custom-call.2 | solution.py:24
  33.1 5.8 %cholesky.107 = f32[64,64]{1,0:T(8,128)S(1)} custom-call(f32[64,64]{1,0:T(8,128)S(1)} %fusion.40), custom_call_target="Cholesky" | custom-call | tf_op jit(solution)/shard_map/jit(cholesky)/cholesky | solution.py:23
  39.7 0.7 fusion.35
  40.3 4.9 %custom-call.13 = f32[1,64,64]{1,2,0:T(8,128)S(1)} custom-call(f32[1,64,64]{2,1,0:T(8,128)S(1)} %fusion.35), custom_call_target="InvertDiagBlocksLowerTriangular" | custom-call | tf_op jit(solution)/shard_map/triangular_solve/custom-call.2 | solution.py:24
  45.2 1.1 convolution_bitcast_fusion
  46.4 115.2 %all-gather.2.cloned.1.call-done = bf16[8192,384]{1,0:T(8,128)(2,1)} async-done(((bf16[64,384]{1,0:T(8,128)(2,1)}), bf16[8192,384]{1,0:T(8,128)(2,1)}) %all-gather.2.cloned.1.call-update) | async-done | bytes 6291472 | tf_op jit(solution)/shard_map/all_gather | solution.py:153
  161.5 3.0 %fusion.10 = f32[128,128]{0,1:T(8,128)S(1)} fusion(bf16[8192,384]{1,0:T(8,128)(2,1)} %all-gather.2.cloned.1.call-done), kind=kOutput, calls=%fused_computation.12 | convolution fusion | flops 268435456 | bytes 2162688 | tf_op jit(solution)/shard_map/dot_general | solution.py:108
  164.8 5.8 %cholesky.74 = f32[64,64]{1,0:T(8,128)S(1)} custom-call(f32[64,64]{1,0:T(8,128)S(1)} %fusion.46), custom_call_target="Cholesky" | custom-call | tf_op jit(solution)/shard_map/jit(cholesky)/cholesky | solution.py:98
  172.0 4.9 %custom-call.10 = f32[1,64,64]{1,2,0:T(8,128)S(1)} custom-call(f32[1,64,64]{2,1,0:T(8,128)S(1)} %fusion.32), custom_call_target="InvertDiagBlocksLowerTriangular" | custom-call | tf_op jit(solution)/shard_map/triangular_solve/custom-call.0 | solution.py:97
  177.6 5.8 %cholesky.85 = f32[64,64]{1,0:T(8,128)S(1)} custom-call(f32[64,64]{1,0:T(8,128)S(1)} %fusion.44), custom_call_target="Cholesky" | custom-call | tf_op jit(solution)/shard_map/jit(cholesky)/cholesky | solution.py:102
  184.1 0.7 fusion.33
  184.8 4.9 %custom-call.11 = f32[1,64,64]{1,2,0:T(8,128)S(1)} custom-call(f32[1,64,64]{2,1,0:T(8,128)S(1)} %fusion.33), custom_call_target="InvertDiagBlocksLowerTriangular" | custom-call | tf_op jit(solution)/shard_map/triangular_solve/custom-call.0 | solution.py:101
  190.2 2.7 fusion.8
  192.9 1.7 fusion.52
  194.6 1.1 copy.35
  195.7 18.1 %dynamic_update_slice.3 = bf16[8192,384]{1,0:T(8,128)(2,1)} dynamic-update-slice(bf16[8192,384]{1,0:T(8,128)(2,1)} %all-gather.2.cloned.1.call-done, bf16[8192,64]{1,0:T(8,128)(2,1)S(1)} %copy.35, s32[]{:T(128)} %constant.65.clone.1, s32[]{:T(128)} %constant.68.clone.1) | dynamic-update-slice | bytes 2097156 | tf_op jit(solution)/shard_map/dynamic_update_slice | solution.py:166
  213.8 7.1 %fusion = f32[512,384]{0,1:T(8,128)S(1)} fusion(bf16[8192,384]{1,0:T(8,128)(2,1)} %dynamic_update_slice.3, bf16[128,8192]{1,0:T(8,128)(2,1)} %collective-permute-done.2, bf16[128,8192]{1,0:T(8,128)(2,1)} %collective-permute-done.1, bf16[128,8192]{1,0:T(8,128)(2,1)} %collective-permute-done, bf16[128,8192]{1,0:T(8,128)(2,1)} %bitcast.68), kind=kOutput, calls=%fused_computation | convolution fusion | flops 3254779904 | bytes 15466496 | tf_op jit(solution)/shard_map/dot_general | solution.py:170
  221.2 0.7 copy-done.1
  222.8 0.8 constant_dynamic-slice_fusion.k_ref
  223.6 12.6 %shard_map.68 = f32[16,2,512]{2,1,0:T(2,128)} custom-call(bf16[512,2048]{1,0:T(8,128)(2,1)} %bitcast.64, bf16[2,512,256]{2,1,0:T(8,128)(2,1)} %constant_dynamic-slice_fusion.k_ref), custom_call_target="tpu_custom_call" | custom-call | tf_op jit(solution)/shard_map/pallas_call | solution.py:82
  236.2 1.0 reduce_sum.27
  237.2 0.7 broadcast_in_dim.8
  237.9 10.1 %all-to-all-start = ((f32[128,1,2]{2,1,0:T(1,128)}), f32[128,1,2]{2,1,0:T(1,128)S(1)}, u32[]{:S(2)}, u32[]{:S(2)}) async-start(f32[128,1,2]{2,1,0:T(1,128)} %broadcast_in_dim.8), calls=%async_computation | async-start | bytes 131072 | tf_op jit(solution)/shard_map/all_to_all | solution.py:142
  248.0 1.9 convolution_multiply_fusion.1
  250.0 12.9 %all-to-all-done = f32[128,1,2]{2,1,0:T(1,128)S(1)} async-done(((f32[128,1,2]{2,1,0:T(1,128)}), f32[128,1,2]{2,1,0:T(1,128)S(1)}, u32[]{:S(2)}, u32[]{:S(2)}) %all-to-all-start) | async-done | bytes 1056 | tf_op jit(solution)/shard_map/all_to_all | solution.py:142
  263.0 7.7 %all_to_all.12 = f32[4,1,2]{2,1,0:T(1,128)S(1)} all-to-all(f32[4,1,2]{2,1,0:T(1,128)S(1)} %broadcast_in_dim.9), channel_id=1, replica_groups=mesh['fsdp'=128,'seq'=4] {'seq'}, dimensions={0} | all-to-all | bytes 64 | tf_op jit(solution)/shard_map/all_to_all | solution.py:142
  (52 shorter events, 8.6 us)
Async XLA Ops:
  7.2 12.5 %copy-start = (f32[1024,64]{0,1:T(8,128)S(1)}, f32[1024,64]{0,1:T(8,128)}, u32[]{:S(2)}) copy-start(f32[1024,64]{0,1:T(8,128)} %param.14) | copy-start | bytes 786436
  7.2 154.3 %all-gather.2.cloned.1.call-start = ((), (), s32[]{:S(2)}) async-start(), calls=%async_computation.2 | async-start | bytes 6340608 | tf_op jit(solution)/shard_map/all_gather | solution.py:153
  9.5 204.3 %collective-permute-start.2 = (bf16[128,8192]{1,0:T(8,128)(2,1)}, bf16[128,8192]{1,0:T(8,128)(2,1)}, u32[]{:S(2)}, u32[]{:S(2)}) collective-permute-start(bf16[128,8192]{1,0:T(8,128)(2,1)} %bitcast.65), channel_id=1, source_target_pairs={{0,3},{1,0},{2,1},{3,2},{4,7},{5,4},{6,5},{7,6},{8,11},{9,8},{10,9... | collective-permute-start | bytes 6291464 | tf_op jit(solution)/shard_map/ppermute | solution.py:159
  14.7 199.1 %collective-permute-start.1 = (bf16[128,8192]{1,0:T(8,128)(2,1)}, bf16[128,8192]{1,0:T(8,128)(2,1)}, u32[]{:S(2)}, u32[]{:S(2)}) collective-permute-start(bf16[128,8192]{1,0:T(8,128)(2,1)} %bitcast.66), channel_id=1, source_target_pairs={{0,2},{1,3},{2,0},{3,1},{4,6},{5,7},{6,4},{7,5},{8,10},{9,11},{10,... | collective-permute-start | bytes 6291464 | tf_op jit(solution)/shard_map/ppermute | solution.py:159
  17.2 196.6 %collective-permute-start = (bf16[128,8192]{1,0:T(8,128)(2,1)}, bf16[128,8192]{1,0:T(8,128)(2,1)}, u32[]{:S(2)}, u32[]{:S(2)}) collective-permute-start(bf16[128,8192]{1,0:T(8,128)(2,1)} %bitcast.67), channel_id=1, source_target_pairs={{0,1},{1,2},{2,3},{3,0},{4,5},{5,6},{6,7},{7,4},{8,9},{9,10},{10,1... | collective-permute-start | bytes 6291464 | tf_op jit(solution)/shard_map/ppermute | solution.py:159
  220.9 1.0 copy-start.1
  237.9 25.0 %all-to-all-start = ((f32[128,1,2]{2,1,0:T(1,128)}), f32[128,1,2]{2,1,0:T(1,128)S(1)}, u32[]{:S(2)}, u32[]{:S(2)}) async-start(f32[128,1,2]{2,1,0:T(1,128)} %broadcast_in_dim.8), calls=%async_computation | async-start | bytes 131072 | tf_op jit(solution)/shard_map/all_to_all | solution.py:142
Sparse Core Ops, SparseCore 0:
  11.1 150.3 all-gather.1

commit v9 on v8

--- a/solution.py
+++ b/solution.py
@@ -163,13 +163,12 @@
     pieces = whole[:, slice_width:]
     q_u = apply_to_pieces(pieces, map_from_gram(gram_of_pieces(pieces, r)), r)
     q_low = q_u.astype(jnp.bfloat16)
-    both = lax.dynamic_update_slice_in_dim(whole, q_low, slice_width, 1)
 
     col_start = me_seq * slice_width
     v_slice = lax.dynamic_slice_in_dim(q_v, col_start, slice_width, 0)
-    prod = jnp.dot(jnp.concatenate(chunks, axis=0), both, preferred_element_type=jnp.float32)
-    base = prod[:, :slice_width]
-    side = prod[:, slice_width : slice_width + r]
+    x_all = jnp.concatenate(chunks, axis=0)
+    base = jnp.dot(x_all, whole, preferred_element_type=jnp.float32)[:, :slice_width]
+    side = jnp.dot(x_all, q_low, preferred_element_type=jnp.float32)
     offset = 2.0 * highest(side, v_slice.T)
     keys = jnp.stack([base + offset, base - offset]).astype(jnp.bfloat16)
     length = keys.shape[1]

time: 279 us -> 262 us (0.939)
  local copies, waits for them, and re-layouts: 21.9 us -> 3.05 us
    dynamic_update_slice x1 -> x0, local copies, waits for them, and re-layouts: 18.1 us -> none  [local(): both = lax.dynamic_update_slice_in_dim(whole, q_low, slice_width, 1)]
    dot_general x1 -> x2, matrix products: 7.13 us -> 10.9 us  [the longest x1 5.76 us: local(): side = jnp.dot(x_all, q_low, preferred_element_type=jnp.float32)]
  transfers between devices with their start and end apart: 5 -> 5, of which waited for: 2 -> 2; matrix products, arithmetic and copies ran while one was open for 29% -> 22% of each run, Pallas kernels for 0% -> 0%
where the time goes in v9:
time: 262 us
  waiting for transfers between devices  130 us (50%)
  other arithmetic  52.8 us (20%)
  matrix products  21.1 us (8%)
  starting transfers between devices  20.3 us (8%)
  between operations  14.5 us (6%)
  Pallas kernels  12.6 us (5%)
  blocking collectives  7.7 us (3%)
  local copies, waits for them, and re-layouts  3.05 us (1%)
    all_gather x1, waiting for transfers between devices, local(): whole = lax.all_gather(packed, 'fsdp', axis=0, tiled=True)  116 us
    all_to_all x1, waiting for transfers between devices, total_over(): return jnp.sum(lax.all_to_all(spread, axis, 0, 0, tiled=True), axis=0)  13.7 us
    another operation x6, other arithmetic, solve_rows(): lower = jnp.linalg.cholesky(gram)  13 us
    pallas_call x1, Pallas kernels, lse_rows(): pl.pallas_call(kern, grid=(kv,), in_specs=[pl.BlockSpec((length, GROUP *...  12.6 us
    another operation x4, other arithmetic, solve_rows(): lax.linalg.triangular_solve(lower, rows, left_side=False, lower=True, tra...  11.1 us
    ppermute x3, starting transfers between devices, local(): lax.ppermute(x_local, 'seq', [(i, (i + shift) % n_seq) for i in range(n_s...  10.2 us
    all_to_all x1, starting transfers between devices, total_over(): return jnp.sum(lax.all_to_all(spread, axis, 0, 0, tiled=True), axis=0)  10.1 us
    all_to_all x1, blocking collectives, total_over(): return jnp.sum(lax.all_to_all(spread, axis, 0, 0, tiled=True), axis=0)  7.7 us
  transfers between devices with their start and end apart: 5, of which 2 were waited for; matrix products, arithmetic and copies ran while one was open for 22% of the time, Pallas kernels for 0%

profile of v9, /device:TPU:1, one launch (start us, length us, event | category | flops | bytes accessed | tf_op | source)
XLA Modules:
  0.0 261.9 jit_solution(12759906687165068847)
XLA Ops:
  7.2 0.8 reduce-precision_convert_fusion.2
  8.0 1.5 pad_maximum_fusion.4
  9.5 5.2 %collective-permute-start.2 = (bf16[128,8192]{1,0:T(8,128)(2,1)}, bf16[128,8192]{1,0:T(8,128)(2,1)}, u32[]{:S(2)}, u32[]{:S(2)}) collective-permute-start(bf16[128,8192]{1,0:T(8,128)(2,1)} %bitcast.67), channel_id=1, source_target_pairs={{0,3},{1,0},{2,1},{3,2},{4,7},{5,4},{6,5},{7,6},{8,11},{9,8},{10,9... | collective-permute-start | bytes 6291464 | tf_op jit(solution)/shard_map/ppermute | solution.py:159
  14.7 2.4 collective-permute-start.1
  17.2 2.5 collective-permute-start
  20.2 5.8 %cholesky.96 = f32[64,64]{1,0:T(8,128)S(1)} custom-call(f32[64,64]{1,0:T(8,128)S(1)} %fusion.37), custom_call_target="Cholesky" | custom-call | tf_op jit(solution)/shard_map/jit(cholesky)/cholesky | solution.py:23
  26.1 0.6 compare_reduce_fusion.1
  26.7 0.7 fusion.29
  27.4 4.9 %custom-call.12 = f32[1,64,64]{1,2,0:T(8,128)S(1)} custom-call(f32[1,64,64]{2,1,0:T(8,128)S(1)} %fusion.29), custom_call_target="InvertDiagBlocksLowerTriangular" | custom-call | tf_op jit(solution)/shard_map/triangular_solve/custom-call.2 | solution.py:24
  33.1 5.8 %cholesky.107 = f32[64,64]{1,0:T(8,128)S(1)} custom-call(f32[64,64]{1,0:T(8,128)S(1)} %fusion.35), custom_call_target="Cholesky" | custom-call | tf_op jit(solution)/shard_map/jit(cholesky)/cholesky | solution.py:23
  39.7 0.7 fusion.30
  40.3 4.9 %custom-call.13 = f32[1,64,64]{1,2,0:T(8,128)S(1)} custom-call(f32[1,64,64]{2,1,0:T(8,128)S(1)} %fusion.30), custom_call_target="InvertDiagBlocksLowerTriangular" | custom-call | tf_op jit(solution)/shard_map/triangular_solve/custom-call.2 | solution.py:24
  45.7 116.2 %all-gather.2.cloned.1.call-done = bf16[8192,384]{1,0:T(8,128)(2,1)} async-done(((bf16[64,384]{1,0:T(8,128)(2,1)}), bf16[8192,384]{1,0:T(8,128)(2,1)}) %all-gather.2.cloned.1.call-update) | async-done | bytes 6291472 | tf_op jit(solution)/shard_map/all_gather | solution.py:153
  161.8 3.0 %fusion.4 = f32[128,128]{0,1:T(8,128)S(1)} fusion(bf16[8192,384]{1,0:T(8,128)(2,1)} %all-gather.2.cloned.1.call-done), kind=kOutput, calls=%fused_computation.7 | convolution fusion | flops 268435456 | bytes 2162688 | tf_op jit(solution)/shard_map/dot_general | solution.py:108
  165.1 5.8 %cholesky.74 = f32[64,64]{1,0:T(8,128)S(1)} custom-call(f32[64,64]{1,0:T(8,128)S(1)} %fusion.41), custom_call_target="Cholesky" | custom-call | tf_op jit(solution)/shard_map/jit(cholesky)/cholesky | solution.py:98
  171.6 0.7 fusion.27
  172.3 4.9 %custom-call.10 = f32[1,64,64]{1,2,0:T(8,128)S(1)} custom-call(f32[1,64,64]{2,1,0:T(8,128)S(1)} %fusion.27), custom_call_target="InvertDiagBlocksLowerTriangular" | custom-call | tf_op jit(solution)/shard_map/triangular_solve/custom-call.0 | solution.py:97
  177.9 5.8 %cholesky.85 = f32[64,64]{1,0:T(8,128)S(1)} custom-call(f32[64,64]{1,0:T(8,128)S(1)} %fusion.39), custom_call_target="Cholesky" | custom-call | tf_op jit(solution)/shard_map/jit(cholesky)/cholesky | solution.py:102
  184.5 0.7 fusion.28
  185.1 4.9 %custom-call.11 = f32[1,64,64]{1,2,0:T(8,128)S(1)} custom-call(f32[1,64,64]{2,1,0:T(8,128)S(1)} %fusion.28), custom_call_target="InvertDiagBlocksLowerTriangular" | custom-call | tf_op jit(solution)/shard_map/triangular_solve/custom-call.0 | solution.py:101
  190.6 2.7 %fusion.2 = f32[8192,192]{0,1:T(8,128)S(1)} fusion(bf16[8192,384]{1,0:T(8,128)(2,1)} %all-gather.2.cloned.1.call-done, bf16[64,64]{1,0:T(8,128)(2,1)S(1)} %broadcast_in_dim.7, bf16[64,64]{1,0:T(8,128)(2,1)S(1)} %get-tuple-element.10, bf16[64,64]{1,0:T(8,128)(2,1)S(1)} %get-tuple-element.11, bf16[64,64]{1,0:T(8,128)(2,1)S(1)} %get-tuple-element.9), kind=kOutput, calls=%fused_computation.5 | convolution fusion | flops 402948096 | bytes 8421376 | tf_op jit(solution)/shard_map/dot_general | solution.py:127
  193.6 1.2 copy-done.1
  194.8 5.8 %fusion.6 = f32[512,64]{0,1:T(8,128)S(1)} fusion(bf16[128,8192]{1,0:T(8,128)(2,1)} %collective-permute-done.2, bf16[128,8192]{1,0:T(8,128)(2,1)} %collective-permute-done.1, bf16[128,8192]{1,0:T(8,128)(2,1)} %collective-permute-done, bf16[128,8192]{1,0:T(8,128)(2,1)S(1)} %bitcast.70, f32[8192,64]{0,1:T(8,128)S(1)} %slice_add_fusion), kind=kOutput, calls=%fused_computation.9 | convolution fusion | flops 570949632 | bytes 10616832 | tf_op jit(solution)/shard_map/dot_general | solution.py:171
  201.3 5.1 %fusion.8 = (bf16[1,512,256]{2,1,0:T(8,128)(2,1)S(1)}, bf16[1,512,256]{2,1,0:T(8,128)(2,1)S(1)}) fusion(f32[512,256]{1,0:T(8,128)S(1)} %convolution_multiply_fusion, bf16[8192,384]{1,0:T(8,128)(2,1)S(1)} %bitcast.66, bf16[128,8192]{1,0:T(8,128)(2,1)} %collective-permute-done.2, bf16[128,8192]{1,0:T(8,128)(2,1)} %collective-permute-done.1, ...), kind=kOutput, calls=%fused_computation.25 | convolution fusion | flops 2181562368 | bytes 13631488 | tf_op jit(solution)/shard_map/dot_general | solution.py:170
  206.6 0.8 constant_dynamic-slice_fusion.k_ref
  207.4 12.6 %shard_map.68 = f32[16,2,512]{2,1,0:T(2,128)} custom-call(bf16[512,2048]{1,0:T(8,128)(2,1)} %bitcast.64, bf16[2,512,256]{2,1,0:T(8,128)(2,1)} %constant_dynamic-slice_fusion.k_ref), custom_call_target="tpu_custom_call" | custom-call | tf_op jit(solution)/shard_map/pallas_call | solution.py:82
  220.0 1.0 reduce_sum.27
  221.0 0.7 broadcast_in_dim.8
  221.7 10.1 %all-to-all-start = ((f32[128,1,2]{2,1,0:T(1,128)}), f32[128,1,2]{2,1,0:T(1,128)S(1)}, u32[]{:S(2)}, u32[]{:S(2)}) async-start(f32[128,1,2]{2,1,0:T(1,128)} %broadcast_in_dim.8), calls=%async_computation | async-start | bytes 131072 | tf_op jit(solution)/shard_map/all_to_all | solution.py:142
  231.8 1.2 convolution_multiply_fusion.1
  233.0 13.7 %all-to-all-done = f32[128,1,2]{2,1,0:T(1,128)S(1)} async-done(((f32[128,1,2]{2,1,0:T(1,128)}), f32[128,1,2]{2,1,0:T(1,128)S(1)}, u32[]{:S(2)}, u32[]{:S(2)}) %all-to-all-start) | async-done | bytes 1056 | tf_op jit(solution)/shard_map/all_to_all | solution.py:142
  246.8 7.7 %all_to_all.12 = f32[4,1,2]{2,1,0:T(1,128)S(1)} all-to-all(f32[4,1,2]{2,1,0:T(1,128)S(1)} %broadcast_in_dim.9), channel_id=1, replica_groups=mesh['fsdp'=128,'seq'=4] {'seq'}, dimensions={0} | all-to-all | bytes 64 | tf_op jit(solution)/shard_map/all_to_all | solution.py:142
  (53 shorter events, 7.1 us)
Async XLA Ops:
  7.2 12.5 %copy-start = (f32[1024,64]{0,1:T(8,128)S(1)}, f32[1024,64]{0,1:T(8,128)}, u32[]{:S(2)}) copy-start(f32[1024,64]{0,1:T(8,128)} %param.14) | copy-start | bytes 786436
  7.2 154.7 %all-gather.2.cloned.1.call-start = ((), (), s32[]{:S(2)}) async-start(), calls=%async_computation.2 | async-start | bytes 6340608 | tf_op jit(solution)/shard_map/all_gather | solution.py:153
  9.5 184.1 %collective-permute-start.2 = (bf16[128,8192]{1,0:T(8,128)(2,1)}, bf16[128,8192]{1,0:T(8,128)(2,1)}, u32[]{:S(2)}, u32[]{:S(2)}) collective-permute-start(bf16[128,8192]{1,0:T(8,128)(2,1)} %bitcast.67), channel_id=1, source_target_pairs={{0,3},{1,0},{2,1},{3,2},{4,7},{5,4},{6,5},{7,6},{8,11},{9,8},{10,9... | collective-permute-start | bytes 6291464 | tf_op jit(solution)/shard_map/ppermute | solution.py:159
  14.7 178.9 %collective-permute-start.1 = (bf16[128,8192]{1,0:T(8,128)(2,1)}, bf16[128,8192]{1,0:T(8,128)(2,1)}, u32[]{:S(2)}, u32[]{:S(2)}) collective-permute-start(bf16[128,8192]{1,0:T(8,128)(2,1)} %bitcast.68), channel_id=1, source_target_pairs={{0,2},{1,3},{2,0},{3,1},{4,6},{5,7},{6,4},{7,5},{8,10},{9,11},{10,... | collective-permute-start | bytes 6291464 | tf_op jit(solution)/shard_map/ppermute | solution.py:159
  17.2 176.4 %collective-permute-start = (bf16[128,8192]{1,0:T(8,128)(2,1)}, bf16[128,8192]{1,0:T(8,128)(2,1)}, u32[]{:S(2)}, u32[]{:S(2)}) collective-permute-start(bf16[128,8192]{1,0:T(8,128)(2,1)} %bitcast.69), channel_id=1, source_target_pairs={{0,1},{1,2},{2,3},{3,0},{4,5},{5,6},{6,7},{7,4},{8,9},{9,10},{10,1... | collective-permute-start | bytes 6291464 | tf_op jit(solution)/shard_map/ppermute | solution.py:159
  193.2 1.6 copy-start.1
  193.2 8.0 %slice-start = ((s8[6291456]{0:T(1024)(128)(4,1)}), s8[4194304]{0:T(1024)(128)(4,1)S(1)}, s32[]{:S(2)}) async-start(s8[6291456]{0:T(1024)(128)(4,1)} %bitcast.65), calls=%async_computation.3 | async-start | bytes 8388608
  193.6 7.7 %slice-start.1 = ((s8[6291456]{0:T(1024)(128)(4,1)}), s8[2097152]{0:T(1024)(128)(4,1)S(1)}, s32[]{:S(2)}) async-start(s8[6291456]{0:T(1024)(128)(4,1)} %bitcast.65), calls=%async_computation.4 | async-start | bytes 4194304
  221.7 25.0 %all-to-all-start = ((f32[128,1,2]{2,1,0:T(1,128)}), f32[128,1,2]{2,1,0:T(1,128)S(1)}, u32[]{:S(2)}, u32[]{:S(2)}) async-start(f32[128,1,2]{2,1,0:T(1,128)} %broadcast_in_dim.8), calls=%async_computation | async-start | bytes 131072 | tf_op jit(solution)/shard_map/all_to_all | solution.py:142
Sparse Core Ops, SparseCore 0:
  11.7 150.1 all-gather.1
